TPU v7x, 512 devices: a whole 4x8x8 slice. The times are simulated.
512 devices in a mesh: dp: 2 (over core), section: 4 (over x), expert: 64 (over y, z).
Axes of the slice: x: 4, y: 8, z: 8, core: 2. Of those that a mesh axis runs over, the one named last changes fastest.
Arguments:
- grad_out: bfloat16 [16384, 3584], P(('dp', 'expert'), 'section'), may hold values from -6 to 6
- expert_ids: int32 [16384, 8], P(('dp', 'expert')), may hold values from 0 to 63, all different within a row; in each aligned block of 128 rows (0 to 127, 128 to 255, ...) at most 24 rows name the same one
- gate_weights: float32 [16384, 8], P(('dp', 'expert')), may hold values from 0.1 to 1
- act: bfloat16 [16384, 8, 1024], P(('dp', 'expert'), None, 'section'), may hold values from -0.8984375 to 0.8984375
- w_down: bfloat16 [64, 1024, 3584], P('expert', 'section'), may hold values from -0.09375 to 0.09375
Outputs:
- grad_hidden: bfloat16 [16384, 8, 1024], P(('dp', 'expert'), None, 'section')
- grad_gates: float32 [16384, 8], P(('dp', 'expert'))
- grad_w: bfloat16 [64, 1024, 3584], P('expert', 'section', 'dp')
Inputs may be any that keep to these rules, and one draw needn't show every extreme that they name: `expert_ids`: each row names 8 different experts. In each aligned block of 128 rows (the tokens of one device) no expert is named by more than 24 rows, and in every draw some expert is named by exactly 24 rows of some block.
All inputs are finite; a program needn't handle non-finite values.
Results may differ from a plain program's by a relative error of at most 0.0058.
Values may be sent and summed in bfloat16 or wider, within the bound.
No kernel may reach another device: no remote copies, remote signals or barrier semaphores. Data moves between devices by JAX's collectives and lax.ppermute only.
A program may use at most 64 MiB of HBM per device.

v0:
```python
import jax
import jax.numpy as jnp
from jax import lax
from jax.sharding import PartitionSpec as P


def arrange(received, n_expert, exp_dev):
    capacity = received.shape[1]
    width = received.shape[2]
    grouped = received.reshape(n_expert, exp_dev, capacity, width)
    return jnp.transpose(grouped, (1, 0, 2, 3)).reshape(exp_dev, n_expert * capacity, width)


def local(grad_out, expert_ids, gate_weights, act, w_down):
    tok_count, top_count = expert_ids.shape
    hidden_slice = act.shape[2]
    exp_dev = w_down.shape[0]
    n_expert = lax.axis_size("expert")
    experts = exp_dev * n_expert
    capacity = 3 * tok_count * top_count // (2 * experts)
    pair_count = tok_count * top_count
    targets = expert_ids.reshape(pair_count)
    onehot = (targets[:, None] == jnp.arange(experts, dtype=jnp.int32)[None, :]).astype(jnp.int32)
    order_in = jnp.sum((jnp.cumsum(onehot, axis=0) - onehot) * onehot, axis=1)
    position = targets * capacity + order_in
    source = (
        jnp.full((experts * capacity,), pair_count, jnp.int32)
        .at[position]
        .set(jnp.arange(pair_count, dtype=jnp.int32))
    )
    filled = source < pair_count
    token_index = jnp.where(filled, source // top_count, tok_count)
    scaled = (
        (gate_weights[:, :, None] * act.astype(jnp.float32))
        .astype(jnp.bfloat16)
        .reshape(pair_count, hidden_slice)
    )
    scaled_ext = jnp.concatenate([scaled, jnp.zeros((1, hidden_slice), jnp.bfloat16)], axis=0)
    send_scaled = scaled_ext[jnp.where(filled, source, pair_count)].reshape(
        experts, capacity, hidden_slice
    )
    full_rows = lax.all_gather(grad_out, "section", axis=1, tiled=True)
    rows_ext = jnp.concatenate(
        [full_rows, jnp.zeros((1, full_rows.shape[1]), jnp.bfloat16)], axis=0
    )
    send_grad = rows_ext[token_index].reshape(experts, capacity, full_rows.shape[1])
    recv_grad, recv_scaled = (
        lax.all_to_all(send_grad, "expert", split_axis=0, concat_axis=0, tiled=True),
        lax.all_to_all(send_scaled, "expert", split_axis=0, concat_axis=0, tiled=True),
    )
    recv_grad = arrange(recv_grad, n_expert, exp_dev)
    recv_scaled = arrange(recv_scaled, n_expert, exp_dev)
    unscaled = jnp.einsum("erd,ehd->erh", recv_grad, w_down, preferred_element_type=jnp.float32)
    weight_part = jnp.einsum(
        "erh,erd->ehd", recv_scaled, recv_grad, preferred_element_type=jnp.float32
    )
    grad_w = lax.psum_scatter(
        weight_part.astype(jnp.bfloat16), "dp", scatter_dimension=2, tiled=True
    )
    returning = unscaled.astype(jnp.bfloat16).reshape(exp_dev, n_expert, capacity, hidden_slice)
    returning = jnp.transpose(returning, (1, 0, 2, 3)).reshape(experts, capacity, hidden_slice)
    returned = lax.all_to_all(returning, "expert", split_axis=0, concat_axis=0, tiled=True)
    unscaled_tok = returned.reshape(experts * capacity, hidden_slice)[position].reshape(
        tok_count, top_count, hidden_slice
    )
    grad_hidden = (gate_weights[:, :, None] * unscaled_tok.astype(jnp.float32)).astype(jnp.bfloat16)
    gate_share = jnp.sum(act.astype(jnp.float32) * unscaled_tok.astype(jnp.float32), axis=2)
    grad_gates = lax.psum(gate_share, "section")
    return (grad_hidden, grad_gates, grad_w)


def solution(mesh):
    placed = (
        P(("dp", "expert"), "section"),
        P(("dp", "expert"), None),
        P(("dp", "expert"), None),
        P(("dp", "expert"), None, "section"),
        P("expert", "section", None),
    )
    return jax.shard_map(
        local,
        mesh=mesh,
        in_specs=placed,
        out_specs=(
            P(("dp", "expert"), None, "section"),
            P(("dp", "expert"), None),
            P("expert", "section", "dp"),
        ),
        check_vma=False,
    )
```

profile of v0, /device:TPU:16, one launch (start us, length us, event | category | flops | bytes accessed | tf_op | source)
XLA Modules:
  0.0 468.3 jit_solution(8120271990553889577)
XLA Ops:
  7.2 0.0 copy-start
  7.2 0.9 copy.20
  8.1 0.1 eq.29
  8.2 0.1 eq.25
  8.3 0.7 broadcast_multiply_fusion
  9.0 18.0 %reduce-window.6 = s32[64,8,128]{2,1,0:T(8,128)S(1)} reduce-window(s32[64,8,128]{2,1,0:T(8,128)S(1)} %fusion.10, s32[]{:T(128)} %constant.16.clone.1), window={size=1x1x128 pad=0_0x0_0x127_0}, to_apply=%region_0.0 | reduce-window | flops 8323072 | bytes 524292 | tf_op jit(solution)/shard_map/reduce-window
  27.0 0.1 slice.14
  27.1 0.1 copy.22
  27.3 0.1 copy.23
  27.4 0.1 broadcast_add_fusion
  27.6 0.1 copy.19
  27.7 0.1 mul.39
  27.8 0.1 fusion.9
  27.9 4.3 scatter_custom_fusion
  32.2 14.8 %all_gather.3 = bf16[128,3584]{1,0:T(8,128)(2,1)S(1)} all-gather(bf16[128,896]{1,0:T(8,128)(2,1)} %param.5), channel_id=1, replica_groups=mesh['dp'=2,'section'=4,'expert'=64] {'section'}, dimensions={1}, use_global_device_ids=true | all-gather | bytes 1146880 | tf_op jit(solution)/shard_map/all_gather | solution.py:42
  47.1 0.1 concatenate.6
  47.1 9.1 %gather_fusion = bf16[1536,3584]{1,0:T(8,128)(2,1)} fusion(bf16[129,3584]{1,0:T(8,128)(2,1)S(1)} %concatenate.6, s32[2048]{0:T(1024)S(1)} %pad_clamp_fusion.1), kind=kCustom, calls=%fused_computation | custom fusion | bytes 22026240 | tf_op jit(solution)/shard_map/gather | solution.py:46
  56.2 261.4 %all_to_all.15 = bf16[64,24,3584]{2,1,0:T(8,128)(2,1)S(1)} all-to-all(bf16[64,24,3584]{2,1,0:T(8,128)(2,1)} %bitcast.46), channel_id=1, replica_groups=mesh['dp'=2,'section'=4,'expert'=64] {'expert'}, dimensions={0} | all-to-all | bytes 22020096 | tf_op jit(solution)/shard_map/all_to_all | solution.py:48
  317.7 4.2 copy-done.1
  321.8 4.1 convolution_convert_fusion
  325.9 31.9 %all-to-all-start.1 = ((bf16[64,24,256]{2,1,0:T(8,128)(2,1)}), bf16[64,24,256]{2,1,0:T(8,128)(2,1)S(1)}, u32[]{:S(2)}, u32[]{:S(2)}) async-start(bf16[64,24,256]{2,1,0:T(8,128)(2,1)} %bitcast.7), calls=%async_computation.1 | async-start | bytes 1572864 | tf_op jit(solution)/shard_map/all_to_all | solution.py:62
  357.8 0.0 reduce-scatter.2.cloned.1.call-start
  357.9 0.1 copy.18
  358.0 23.1 %all-to-all-done.1 = bf16[64,24,256]{2,1,0:T(8,128)(2,1)S(1)} async-done(((bf16[64,24,256]{2,1,0:T(8,128)(2,1)}), bf16[64,24,256]{2,1,0:T(8,128)(2,1)S(1)}, u32[]{:S(2)}, u32[]{:S(2)}) %all-to-all-start.1) | async-done | bytes 786464 | tf_op jit(solution)/shard_map/all_to_all | solution.py:62
  381.1 3.9 gather_fusion.1
  385.0 2.2 fusion.6
  387.3 4.8 %gather_fusion.2 = bf16[1536,256]{1,0:T(8,128)(2,1)S(1)} fusion(bf16[1025,256]{1,0:T(8,128)(2,1)S(1)} %concatenate.7, s32[2048]{0:T(1024)S(1)} %pad_clamp_fusion), kind=kCustom, calls=%fused_computation.2 | custom fusion | bytes 1579008 | tf_op jit(solution)/shard_map/gather | solution.py:39
  392.1 28.1 %all_to_all.16 = bf16[64,24,256]{2,1,0:T(8,128)(2,1)S(1)} all-to-all(bf16[64,24,256]{2,1,0:T(8,128)(2,1)S(1)} %bitcast.48), channel_id=1, replica_groups=mesh['dp'=2,'section'=4,'expert'=64] {'expert'}, dimensions={0} | all-to-all | bytes 1572864 | tf_op jit(solution)/shard_map/all_to_all | solution.py:49
  420.2 8.3 %fusion.1 = bf16[1,256,3584]{2,1,0:T(8,128)(2,1)} fusion(bf16[64,24,256]{2,1,0:T(8,128)(2,1)S(1)} %all_to_all.16, bf16[64,24,3584]{2,1,0:T(8,128)(2,1)} %copy-done.1), kind=kOutput, calls=%fused_computation.6 | convolution fusion | flops 2819489792 | bytes 13631488 | tf_op jit(solution)/shard_map/erh,erd->ehd/dot_general | solution.py:54
  428.6 0.0 reduce-scatter.2.cloned.1.call-update
  428.6 32.2 %psum.7 = f32[128,8]{1,0:T(8,128)S(1)} all-reduce(f32[128,8]{1,0:T(8,128)S(1)} %get-tuple-element.7), channel_id=1, replica_groups=mesh['dp'=2,'section'=4,'expert'=64] {'section'}, use_global_device_ids=true, to_apply=%region_5.6 | all-reduce | flops 1024 | bytes 8192 | tf_op jit(solution)/shard_map/psum | solution.py:68
  460.8 0.7 copy.26
  (15 shorter events, 0.1 us)
Async XLA Ops:
  7.2 314.7 %copy-start = (bf16[1,256,3584]{2,1,0:T(8,128)(2,1)S(1)}, bf16[1,256,3584]{2,1,0:T(8,128)(2,1)}, u32[]{:S(2)}) copy-start(bf16[1,256,3584]{2,1,0:T(8,128)(2,1)} %param.9) | copy-start | bytes 5505028
  317.7 4.2 copy-start.1
  317.7 40.2 %copy-start.2 = (f32[128,8]{0,1:T(8,128)S(1)}, f32[128,8]{0,1:T(8,128)}, u32[]{:S(2)}) copy-start(f32[128,8]{0,1:T(8,128)} %param.7) | copy-start | bytes 12292
  325.9 55.2 %all-to-all-start.1 = ((bf16[64,24,256]{2,1,0:T(8,128)(2,1)}), bf16[64,24,256]{2,1,0:T(8,128)(2,1)S(1)}, u32[]{:S(2)}, u32[]{:S(2)}) async-start(bf16[64,24,256]{2,1,0:T(8,128)(2,1)} %bitcast.7), calls=%async_computation.1 | async-start | bytes 1572864 | tf_op jit(solution)/shard_map/all_to_all | solution.py:62
  357.8 103.6 %reduce-scatter.2.cloned.1.call-start = ((), (), s32[]{:S(2)}) async-start(), calls=%async_computation.4 | async-start | bytes 2752512 | tf_op jit(solution)/shard_map/reduce_scatter | solution.py:57
Sparse Core Ops, SparseCore 0:
  428.7 28.0 reduce-scatter.1
where the time goes:
time: 469 us; the launch traced here: 468 us
  blocking collectives  337 us (72%)
  starting transfers between devices  31.9 us (7%)
  local copies, waits for them, and re-layouts  28.8 us (6%)
  waiting for transfers between devices  23.1 us (5%)
  other arithmetic  21.2 us (5%)
  between operations  14.2 us (3%)
  matrix products  12.4 us (3%)
    all_to_all x1, blocking collectives, local(): lax.all_to_all(send_grad, 'expert', split_axis=0, concat_axis=0, tiled=True)  261 us
    psum x1, blocking collectives, local(): grad_gates = lax.psum(gate_share, 'section')  32.2 us
    all_to_all x1, starting transfers between devices, local(): lax.all_to_all(returning, 'expert', split_axis=0, concat_axis=0, tiled=True)  31.9 us
    all_to_all x1, blocking collectives, local(): lax.all_to_all(send_scaled, 'expert', split_axis=0, concat_axis=0, tiled=...  28.1 us
    all_to_all x1, waiting for transfers between devices, local(): lax.all_to_all(returning, 'expert', split_axis=0, concat_axis=0, tiled=True)  23.1 us
    another operation x3, other arithmetic  18.2 us
    all_gather x1, blocking collectives, local(): full_rows = lax.all_gather(grad_out, 'section', axis=1, tiled=True)  14.8 us
  transfers between devices with their start and end apart: 2, of which 1 were waited for; matrix products, arithmetic and copies ran while one was open for 0% of the time, Pallas kernels for 0%

commit v1 on v0

v1 whole, which is shorter than its diff:
```python
import jax
import jax.numpy as jnp
from jax import lax
from jax.sharding import PartitionSpec as P


def routing(expert_ids, experts, capacity):
    tok_count, top_count = expert_ids.shape
    onehot = expert_ids[:, :, None] == jnp.arange(experts, dtype=jnp.int32)[None, None, :]
    per_token = jnp.any(onehot, axis=1).astype(jnp.bfloat16)
    rows = jnp.arange(tok_count, dtype=jnp.int32)
    lower = (rows[:, None] > rows[None, :]).astype(jnp.bfloat16)
    before = jnp.dot(lower, per_token, preferred_element_type=jnp.float32)
    order_in = jnp.sum(jnp.where(onehot, before[:, None, :], 0.0), axis=2).astype(jnp.int32)
    position = expert_ids * capacity + order_in
    slots = jnp.arange(experts * capacity, dtype=jnp.int32)
    sel_pairs = position.reshape(tok_count * top_count)[None, :] == slots[:, None]
    sel_tok = jnp.any(position[None, :, :] == slots[:, None, None], axis=2)
    return sel_pairs.astype(jnp.bfloat16), sel_tok.astype(jnp.bfloat16)


def local(grad_out, expert_ids, gate_weights, act, w_down):
    tok_count, top_count = expert_ids.shape
    hidden_slice = act.shape[2]
    d_slice = grad_out.shape[1]
    n_expert = lax.axis_size("expert")
    n_section = lax.axis_size("section")
    experts = w_down.shape[0] * n_expert
    capacity = 3 * tok_count * top_count // (2 * experts)
    pair_count = tok_count * top_count
    slot_count = experts * capacity

    sel_pairs, sel_tok = routing(expert_ids, experts, capacity)
    scaled = (
        (gate_weights[:, :, None] * act.astype(jnp.float32))
        .astype(jnp.bfloat16)
        .reshape(pair_count, hidden_slice)
    )
    send_scaled = jnp.dot(sel_pairs, scaled, preferred_element_type=jnp.float32).astype(jnp.bfloat16)
    send_grad = jnp.dot(sel_tok, grad_out, preferred_element_type=jnp.float32).astype(jnp.bfloat16)
    send = jnp.concatenate([send_grad, send_scaled], axis=1).reshape(
        experts, capacity, d_slice + hidden_slice
    )
    recv = lax.all_to_all(send, "expert", split_axis=0, concat_axis=0, tiled=True)
    recv = recv.reshape(slot_count, d_slice + hidden_slice)
    recv_grad = recv[:, :d_slice]
    recv_scaled = recv[:, d_slice:]
    spread = jnp.broadcast_to(recv_grad[None], (n_section, slot_count, d_slice))
    gathered = lax.all_to_all(spread, "section", split_axis=0, concat_axis=0, tiled=True)
    w_local = w_down[0].reshape(hidden_slice, n_section, d_slice)
    unscaled = jnp.einsum("srd,hsd->rh", gathered, w_local, preferred_element_type=jnp.float32)
    weight_part = jnp.einsum(
        "rh,srd->hsd", recv_scaled, gathered, preferred_element_type=jnp.float32
    ).astype(jnp.bfloat16).reshape(1, hidden_slice, n_section * d_slice)
    grad_w = lax.psum_scatter(weight_part, "dp", scatter_dimension=2, tiled=True)
    returning = unscaled.astype(jnp.bfloat16).reshape(experts, capacity, hidden_slice)
    returned = lax.all_to_all(returning, "expert", split_axis=0, concat_axis=0, tiled=True)
    unscaled_tok = lax.dot_general(
        sel_pairs,
        returned.reshape(slot_count, hidden_slice),
        (((0,), (0,)), ((), ())),
        preferred_element_type=jnp.float32,
    ).reshape(tok_count, top_count, hidden_slice)
    grad_hidden = (gate_weights[:, :, None] * unscaled_tok).astype(jnp.bfloat16)
    gate_share = jnp.sum(act.astype(jnp.float32) * unscaled_tok, axis=2)
    grad_gates = lax.psum(gate_share, "section")
    return (grad_hidden, grad_gates, grad_w)


def solution(mesh):
    placed = (
        P(("dp", "expert"), "section"),
        P(("dp", "expert"), None),
        P(("dp", "expert"), None),
        P(("dp", "expert"), None, "section"),
        P("expert", "section", None),
    )
    return jax.shard_map(
        local,
        mesh=mesh,
        in_specs=placed,
        out_specs=(
            P(("dp", "expert"), None, "section"),
            P(("dp", "expert"), None),
            P("expert", "section", "dp"),
        ),
        check_vma=False,
    )
```

time: 469 us -> 340 us (0.72)
  blocking collectives: 337 us -> 272 us
  starting transfers between devices: 31.9 us -> 0.04 us
  waiting for transfers between devices: 23.1 us -> 0.02 us
  other arithmetic: 21.2 us -> 10 us
  matrix products: 12.4 us -> 17.1 us
    all_to_all x1 -> x0, starting transfers between devices: 31.9 us -> none  [local(): lax.all_to_all(returning, 'expert', split_axis=0, concat_axis=0, tiled=True)]
    all_to_all x2 -> x3, blocking collectives: 290 us -> 263 us  [the longest x1 125 us: local(): lax.all_to_all(spread, 'section', split_axis=0, concat_axis=0, tiled=True)]
    all_to_all x1 -> x0, waiting for transfers between devices: 23.1 us -> none  [local(): lax.all_to_all(returning, 'expert', split_axis=0, concat_axis=0, tiled=True)]
    psum x1, blocking collectives: 32.2 us -> 9.2 us  [local(): grad_gates = lax.psum(gate_share, 'section')]
    another operation x3 -> x0, other arithmetic: 18.2 us -> none
    gather x3 -> x0, local copies, waits for them, and re-layouts: 17.8 us -> none  [the longest x1 9.09 us: local(): rows_ext[token_index].reshape(experts, capacity, full_rows.shape[1])]
    all_gather x1 -> x0, blocking collectives: 14.8 us -> none  [local(): full_rows = lax.all_gather(grad_out, 'section', axis=1, tiled=True)]
    reduce_or x0 -> x2, other arithmetic: none -> 6.38 us  [the longest x1 5.56 us: routing(): sel_tok = jnp.any(position[None, :, :] == slots[:, None, None], axis=2)]
  transfers between devices with their start and end apart: 2 -> 1, of which waited for: 1 -> 0; matrix products, arithmetic and copies ran while one was open for 0% -> 3% of each run, Pallas kernels for 0% -> 0%
where the time goes in v1:
time: 340 us; the launch traced here: 339 us
  blocking collectives  272 us (80%)
  local copies, waits for them, and re-layouts  25.7 us (8%)
  matrix products  17.1 us (5%)
  between operations  14.1 us (4%)
  other arithmetic  10 us (3%)
    all_to_all x1, blocking collectives, local(): lax.all_to_all(spread, 'section', split_axis=0, concat_axis=0, tiled=True)  125 us
    all_to_all x1, blocking collectives, local(): lax.all_to_all(send, 'expert', split_axis=0, concat_axis=0, tiled=True)  99 us
    all_to_all x1, blocking collectives, local(): lax.all_to_all(returning, 'expert', split_axis=0, concat_axis=0, tiled=True)  38.6 us
    unnamed x14, local copies, waits for them, and re-layouts  9.35 us
    psum x1, blocking collectives, local(): grad_gates = lax.psum(gate_share, 'section')  9.2 us
    dot_general x1, matrix products, local(): jnp.einsum('srd,hsd->rh', gathered, w_local, preferred_element_type=jnp.f...  7.7 us
  transfers between devices with their start and end apart: 1, of which 0 were waited for; matrix products, arithmetic and copies ran while one was open for 3% of the time, Pallas kernels for 0%

profile of v1, /device:TPU:16, one launch (start us, length us, event | category | flops | bytes accessed | tf_op | source)
XLA Modules:
  0.0 339.1 jit_solution(5224360648791601588)
XLA Ops:
  7.2 0.0 copy-start
  7.2 0.0 copy-start.5
  7.2 0.0 copy-start.4
  7.2 0.0 reduce-scatter.2.cloned.1.call-start
  7.2 0.8 fusion.14
  8.1 0.1 fusion.15
  8.2 0.7 select_reduce_fusion
  9.0 0.7 convert_add_fusion
  9.6 5.6 %fusion.3 = pred[1536,128]{1,0:T(8,128)(4,1)S(1)} fusion(s32[128,8]{0,1:T(8,128)S(1)} %convert_add_fusion), kind=kLoop, calls=%fused_computation.5 | loop fusion | flops 2949120 | bytes 200704 | tf_op jit(solution)/shard_map/reduce_or | solution.py:18
  15.2 0.1 copy.27
  15.3 0.1 eq.70
  15.4 0.9 convolution_convert_fusion
  16.4 0.2 fusion.10
  16.6 1.6 fusion.8
  18.2 2.0 pad_maximum_fusion
  20.2 5.8 %copy.30 = bf16[1536,1152]{1,0:T(8,128)(2,1)} copy(bf16[1536,1152]{0,1:T(8,128)(2,1)} %pad_maximum_fusion) | data formatting | bytes 7077888 | tf_op jit(solution)/shard_map/concatenate | solution.py:41
  26.0 99.0 %all_to_all.15 = bf16[64,24,1152]{2,1,0:T(8,128)(2,1)S(1)} all-to-all(bf16[64,24,1152]{2,1,0:T(8,128)(2,1)} %bitcast.29), channel_id=1, replica_groups=mesh['dp'=2,'section'=4,'expert'=64] {'expert'}, dimensions={0} | all-to-all | bytes 7077888 | tf_op jit(solution)/shard_map/all_to_all | solution.py:44
  125.0 1.9 copy-done.1
  126.8 0.2 slice.8
  127.0 5.0 %broadcast_in_dim.16 = bf16[4,1536,896]{2,1,0:T(8,128)(2,1)} broadcast(bf16[1536,896]{1,0:T(8,128)(2,1)S(1)} %slice.8), dimensions={1,2} | broadcast | bytes 13762560 | tf_op jit(solution)/shard_map/broadcast_in_dim | solution.py:48
  132.0 125.3 %all_to_all.16 = bf16[4,1536,896]{2,1,0:T(8,128)(2,1)S(1)} all-to-all(bf16[4,1536,896]{2,1,0:T(8,128)(2,1)} %broadcast_in_dim.16), channel_id=1, replica_groups=mesh['dp'=2,'section'=4,'expert'=64] {'section'}, dimensions={0} | all-to-all | bytes 22020096 | tf_op jit(solution)/shard_map/all_to_all | solution.py:49
  257.4 4.2 %copy-done.2 = bf16[4,1536,896]{2,1,0:T(8,128)(2,1)} copy-done((bf16[4,1536,896]{2,1,0:T(8,128)(2,1)}, bf16[4,1536,896]{2,1,0:T(8,128)(2,1)S(1)}, u32[]{:S(2)}) %copy-start.2) | copy-done | bytes 11010072
  261.5 5.3 %convolution_convert_fusion.1 = bf16[256,4,896]{2,0,1:T(8,128)(2,1)} fusion(bf16[4,1536,896]{2,1,0:T(8,128)(2,1)S(1)} %all_to_all.16, bf16[1536,1152]{1,0:T(8,128)(2,1)} %bitcast.31), kind=kOutput, calls=%fused_computation.15 | convolution fusion | flops 2819489792 | bytes 13631488 | tf_op jit(solution)/shard_map/rh,srd->hsd/dot_general | solution.py:52
  266.8 3.7 %copy.33 = bf16[256,4,896]{0,2,1:T(8,128)(2,1)} copy(bf16[256,4,896]{2,0,1:T(8,128)(2,1)} %convolution_convert_fusion.1) | data formatting | bytes 3670016 | tf_op jit(solution)/shard_map/convert_element_type | solution.py:54
  270.5 0.0 reduce-scatter.2.cloned.1.call-update
  270.6 1.5 reshape_squeeze.3
  272.1 7.7 %fusion.7 = bf16[1536,256]{1,0:T(8,128)(2,1)S(1)} fusion(bf16[4,1536,896]{2,1,0:T(8,128)(2,1)} %copy-done.2, bf16[256,4,896]{2,1,0:T(4,128)(2,1)} %reshape_squeeze.3), kind=kOutput, calls=%fused_computation.12 | convolution fusion | flops 2818965504 | bytes 13631488 | tf_op jit(solution)/shard_map/srd,hsd->rh/dot_general | solution.py:51
  279.8 38.6 %all_to_all.17 = bf16[64,24,256]{2,1,0:T(8,128)(2,1)S(1)} all-to-all(bf16[64,24,256]{2,1,0:T(8,128)(2,1)S(1)} %bitcast.34), channel_id=1, replica_groups=mesh['dp'=2,'section'=4,'expert'=64] {'expert'}, dimensions={0} | all-to-all | bytes 1572864 | tf_op jit(solution)/shard_map/all_to_all | solution.py:57
  318.4 1.4 fusion.11
  319.8 1.1 copy.34
  320.9 9.2 %psum.7 = f32[128,8]{0,1:T(8,128)} all-reduce(f32[128,8]{0,1:T(8,128)S(1)} %get-tuple-element.12), channel_id=1, replica_groups=mesh['dp'=2,'section'=4,'expert'=64] {'section'}, use_global_device_ids=true, to_apply=%region_4.5 | all-reduce | flops 1024 | bytes 8192 | tf_op jit(solution)/shard_map/psum | solution.py:66
  330.1 2.2 copy.35
  (8 shorter events, 0.0 us)
Async XLA Ops:
  7.2 8.3 %copy-start = (bf16[128,896]{1,0:T(8,128)(2,1)S(1)}, bf16[128,896]{1,0:T(8,128)(2,1)}, u32[]{:S(2)}) copy-start(bf16[128,896]{1,0:T(8,128)(2,1)} %param.5) | copy-start | bytes 688132
  7.2 9.2 %copy-start.5 = (f32[128,8]{0,1:T(8,128)S(1)}, f32[128,8]{0,1:T(8,128)}, u32[]{:S(2)}) copy-start(f32[128,8]{0,1:T(8,128)} %param.7) | copy-start | bytes 12292
  7.2 9.2 %copy-start.4 = (bf16[128,8,256]{2,1,0:T(8,128)(2,1)S(1)}, bf16[128,8,256]{2,1,0:T(8,128)(2,1)}, u32[]{:S(2)}) copy-start(bf16[128,8,256]{2,1,0:T(8,128)(2,1)} %param.8) | copy-start | bytes 1572868
  7.2 322.9 %reduce-scatter.2.cloned.1.call-start = ((), (), s32[]{:S(2)}) async-start(), calls=%async_computation.4 | async-start | bytes 2752512 | tf_op jit(solution)/shard_map/reduce_scatter | solution.py:55
  125.0 1.9 copy-start.1
  257.4 4.2 %copy-start.2 = (bf16[4,1536,896]{2,1,0:T(8,128)(2,1)}, bf16[4,1536,896]{2,1,0:T(8,128)(2,1)S(1)}, u32[]{:S(2)}) copy-start(bf16[4,1536,896]{2,1,0:T(8,128)(2,1)S(1)} %all_to_all.16) | copy-start | bytes 33030148
  266.8 3.7 %copy-start.3 = (bf16[1,256,3584]{2,1,0:T(8,128)(2,1)S(1)}, bf16[1,256,3584]{2,1,0:T(8,128)(2,1)}, u32[]{:S(2)}) copy-start(bf16[1,256,3584]{2,1,0:T(8,128)(2,1)} %param.9) | copy-start | bytes 5505028
Sparse Core Ops, SparseCore 0:
  270.7 19.9 reduce-scatter.1

commit v2 on v1

--- a/solution.py
+++ b/solution.py
@@ -41,19 +41,26 @@
     send = jnp.concatenate([send_grad, send_scaled], axis=1).reshape(
         experts, capacity, d_slice + hidden_slice
     )
-    recv = lax.all_to_all(send, "expert", split_axis=0, concat_axis=0, tiled=True)
-    recv = recv.reshape(slot_count, d_slice + hidden_slice)
-    recv_grad = recv[:, :d_slice]
-    recv_scaled = recv[:, d_slice:]
-    spread = jnp.broadcast_to(recv_grad[None], (n_section, slot_count, d_slice))
-    gathered = lax.all_to_all(spread, "section", split_axis=0, concat_axis=0, tiled=True)
     w_local = w_down[0].reshape(hidden_slice, n_section, d_slice)
-    unscaled = jnp.einsum("srd,hsd->rh", gathered, w_local, preferred_element_type=jnp.float32)
-    weight_part = jnp.einsum(
-        "rh,srd->hsd", recv_scaled, gathered, preferred_element_type=jnp.float32
-    ).astype(jnp.bfloat16).reshape(1, hidden_slice, n_section * d_slice)
+    chunks = 2
+    step = capacity // chunks
+    received = []
+    for c in range(chunks):
+        part = lax.all_to_all(
+            send[:, c * step:(c + 1) * step], "expert", split_axis=0, concat_axis=0, tiled=True
+        ).reshape(experts * step, d_slice + hidden_slice)
+        gathered = lax.all_gather(part[:, :d_slice], "section", axis=0, tiled=False)
+        received.append((part[:, d_slice:], gathered))
+    weight_acc = None
+    returning = []
+    for recv_scaled, gathered in received:
+        unscaled = jnp.einsum("srd,hsd->rh", gathered, w_local, preferred_element_type=jnp.float32)
+        returning.append(unscaled.astype(jnp.bfloat16).reshape(experts, step, hidden_slice))
+        term = jnp.einsum("rh,srd->hsd", recv_scaled, gathered, preferred_element_type=jnp.float32)
+        weight_acc = term if weight_acc is None else weight_acc + term
+    weight_part = weight_acc.astype(jnp.bfloat16).reshape(1, hidden_slice, n_section * d_slice)
     grad_w = lax.psum_scatter(weight_part, "dp", scatter_dimension=2, tiled=True)
-    returning = unscaled.astype(jnp.bfloat16).reshape(experts, capacity, hidden_slice)
+    returning = jnp.concatenate(returning, axis=1)
     returned = lax.all_to_all(returning, "expert", split_axis=0, concat_axis=0, tiled=True)
     unscaled_tok = lax.dot_general(
         sel_pairs,

time: 340 us -> 325 us (0.956)
  blocking collectives: 272 us -> 192 us
  waiting for transfers between devices: 0.02 us -> 56.5 us
  matrix products: 17.1 us -> 24.8 us
    all_to_all x2, blocking collectives: 224 us -> 144 us  [local(): lax.all_to_all(send[:, c * step:(c + 1) * step], 'expert', split_axis=0,...]
    all_gather x0 -> x2, waiting for transfers between devices: none -> 56.4 us  [local(): gathered = lax.all_gather(part[:, :d_slice], 'section', axis=0, tiled=False)]
    slice x1 -> x3, local copies, waits for them, and re-layouts: 0.22 us -> 9.76 us  [the longest x2 5.05 us: local(): gathered = lax.all_gather(part[:, :d_slice], 'section', axis=0, tiled=False)]
    dot_general x1 -> x2, matrix products: 5.32 us -> 11.7 us  [local(): jnp.einsum('rh,srd->hsd', recv_scaled, gathered, preferred_element_type=j...]
    broadcast_in_dim x1 -> x0, local copies, waits for them, and re-layouts: 4.98 us -> none  [local(): spread = jnp.broadcast_to(recv_grad[None], (n_section, slot_count, d_slice))]
    unnamed x14 -> x12, local copies, waits for them, and re-layouts: 9.35 us -> 4.8 us
    dot_general x1 -> x2, matrix products: 7.7 us -> 9.06 us  [local(): jnp.einsum('srd,hsd->rh', gathered, w_local, preferred_element_type=jnp.f...]
  transfers between devices with their start and end apart: 1 -> 3, of which waited for: 0 -> 1; matrix products, arithmetic and copies ran while one was open for 3% -> 7% of each run, Pallas kernels for 0% -> 0%
where the time goes in v2:
time: 325 us
  blocking collectives  192 us (59%)
  waiting for transfers between devices  56.5 us (17%)
  local copies, waits for them, and re-layouts  27.5 us (8%)
  matrix products  24.8 us (8%)
  between operations  13.9 us (4%)
  other arithmetic  10.3 us (3%)
    all_to_all x2, blocking collectives, local(): lax.all_to_all(send[:, c * step:(c + 1) * step], 'expert', split_axis=0,...  144 us
    all_gather x2, waiting for transfers between devices, local(): gathered = lax.all_gather(part[:, :d_slice], 'section', axis=0, tiled=False)  56.4 us
    all_to_all x1, blocking collectives, local(): lax.all_to_all(returning, 'expert', split_axis=0, concat_axis=0, tiled=True)  37.8 us
    dot_general x2, matrix products, local(): jnp.einsum('rh,srd->hsd', recv_scaled, gathered, preferred_element_type=j...  11.7 us
    psum x1, blocking collectives, local(): grad_gates = lax.psum(gate_share, 'section')  9.62 us
    dot_general x2, matrix products, local(): jnp.einsum('srd,hsd->rh', gathered, w_local, preferred_element_type=jnp.f...  9.06 us
  transfers between devices with their start and end apart: 3, of which 1 were waited for; matrix products, arithmetic and copies ran while one was open for 7% of the time, Pallas kernels for 0%

profile of v2, /device:TPU:16, one launch (start us, length us, event | category | flops | bytes accessed | tf_op | source)
XLA Modules:
  0.0 324.8 jit_solution(16550532384872335757)
XLA Ops:
  7.2 0.8 fusion.29
  8.1 0.1 fusion.30
  8.2 0.7 select_reduce_fusion
  9.0 0.7 convert_add_fusion
  9.6 5.6 %fusion.3 = pred[1536,128]{1,0:T(8,128)(4,1)S(1)} fusion(s32[128,8]{0,1:T(8,128)S(1)} %convert_add_fusion), kind=kLoop, calls=%fused_computation.5 | loop fusion | flops 2949120 | bytes 200704 | tf_op jit(solution)/shard_map/reduce_or | solution.py:18
  15.4 0.9 convolution_convert_fusion
  16.4 0.2 fusion.24
  16.6 1.6 fusion.7
  18.2 2.0 pad_maximum_fusion
  20.2 5.8 %copy.34 = bf16[1536,1152]{1,0:T(8,128)(2,1)} copy(bf16[1536,1152]{0,1:T(8,128)(2,1)} %pad_maximum_fusion) | data formatting | bytes 7077888 | tf_op jit(solution)/shard_map/concatenate | solution.py:41
  26.0 4.7 %fusion.31 = (bf16[64,12,1152]{2,1,0:T(8,128)(2,1)S(1)}, bf16[64,12,1152]{2,1,0:T(8,128)(2,1)}) fusion(bf16[64,24,1152]{2,1,0:T(8,128)(2,1)} %bitcast.39), kind=kLoop, calls=%fused_computation.38 | loop fusion | bytes 7077888 | tf_op jit(solution)/shard_map/slice | solution.py:50
  30.7 74.4 %all_to_all.15 = bf16[64,12,1152]{2,1,0:T(8,128)(2,1)S(1)} all-to-all(bf16[64,12,1152]{2,1,0:T(8,128)(2,1)S(1)} %get-tuple-element.12), channel_id=1, replica_groups=mesh['dp'=2,'section'=4,'expert'=64] {'expert'}, dimensions={0} | all-to-all | bytes 3538944 | tf_op jit(solution)/shard_map/all_to_all | solution.py:49
  105.1 1.4 reshape.54
  106.5 2.5 slice.25
  109.1 69.7 %all_to_all.16 = bf16[64,12,1152]{2,1,0:T(8,128)(2,1)S(1)} all-to-all(bf16[64,12,1152]{2,1,0:T(8,128)(2,1)} %get-tuple-element.13), channel_id=1, replica_groups=mesh['dp'=2,'section'=4,'expert'=64] {'expert'}, dimensions={0} | all-to-all | bytes 3538944 | tf_op jit(solution)/shard_map/all_to_all | solution.py:49
  178.8 1.4 reshape.56
  180.2 2.5 slice.27
  182.8 0.2 reduce-scatter.2.cloned.1.call-start
  183.1 6.2 %fusion.28 = f32[256,4,896]{2,0,1:T(8,128)} fusion(bf16[4,768,896]{2,1,0:T(8,128)(2,1)} %bitcast.41, bf16[768,1152]{1,0:T(8,128)(2,1)} %reshape.54), kind=kOutput, calls=%fused_computation.31 | convolution fusion | flops 1409286144 | bytes 9568256 | tf_op jit(solution)/shard_map/rh,srd->hsd/dot_general | solution.py:59
  189.3 56.4 %all-gather.7.cloned.1.call-done = bf16[3072,896]{1,0:T(8,128)(2,1)} async-done(((bf16[768,896]{1,0:T(8,128)(2,1)}), bf16[3072,896]{1,0:T(8,128)(2,1)}) %all-gather.7.cloned.1.call-update) | async-done | bytes 5505040 | tf_op jit(solution)/shard_map/all_gather | solution.py:52
  245.7 5.4 %add_convert_fusion = bf16[256,4,896]{2,0,1:T(8,128)(2,1)S(1)} fusion(f32[256,4,896]{2,0,1:T(8,128)} %fusion.28, bf16[4,768,896]{2,1,0:T(8,128)(2,1)} %bitcast.43, bf16[768,1152]{1,0:T(8,128)(2,1)} %reshape.56), kind=kOutput, calls=%fused_computation.7 | convolution fusion | flops 1411121152 | bytes 11403264 | tf_op jit(solution)/shard_map/rh,srd->hsd/dot_general | solution.py:59
  251.1 2.4 copy.39
  253.6 1.5 copy-done.1
  255.1 1.5 reshape_squeeze.3
  256.6 4.9 %fusion.21 = bf16[768,256]{1,0:T(8,128)(2,1)S(1)} fusion(bf16[4,768,896]{2,1,0:T(8,128)(2,1)} %bitcast.42, bf16[256,4,896]{2,1,0:T(4,128)(2,1)} %reshape_squeeze.3), kind=kOutput, calls=%fused_computation.22 | convolution fusion | flops 1409482752 | bytes 7733248 | tf_op jit(solution)/shard_map/srd,hsd->rh/dot_general | solution.py:57
  261.5 4.2 %fusion.18 = bf16[768,256]{1,0:T(8,128)(2,1)S(1)} fusion(bf16[4,768,896]{2,1,0:T(8,128)(2,1)} %bitcast.44, bf16[256,4,896]{2,1,0:T(4,128)(2,1)S(1)} %copy-done.2), kind=kOutput, calls=%fused_computation.21 | convolution fusion | flops 1409482752 | bytes 7733248 | tf_op jit(solution)/shard_map/srd,hsd->rh/dot_general | solution.py:57
  265.8 0.3 pad_maximum_fusion.1
  266.1 37.8 %all_to_all.17 = bf16[64,24,256]{2,1,0:T(8,128)(2,1)S(1)} all-to-all(bf16[64,24,256]{2,1,0:T(8,128)(2,1)S(1)} %pad_maximum_fusion.1), channel_id=1, replica_groups=mesh['dp'=2,'section'=4,'expert'=64] {'expert'}, dimensions={0} | all-to-all | bytes 1572864 | tf_op jit(solution)/shard_map/all_to_all | solution.py:64
  303.9 1.4 fusion.25
  305.3 1.1 copy.40
  306.4 9.6 %psum.7 = f32[128,8]{0,1:T(8,128)} all-reduce(f32[128,8]{0,1:T(8,128)S(1)} %get-tuple-element.14), channel_id=1, replica_groups=mesh['dp'=2,'section'=4,'expert'=64] {'section'}, use_global_device_ids=true, to_apply=%region_4.5 | all-reduce | flops 1024 | bytes 8192 | tf_op jit(solution)/shard_map/psum | solution.py:73
  316.0 2.2 copy.41
  (20 shorter events, 0.5 us)
Async XLA Ops:
  7.2 8.3 %copy-start = (bf16[128,896]{1,0:T(8,128)(2,1)S(1)}, bf16[128,896]{1,0:T(8,128)(2,1)}, u32[]{:S(2)}) copy-start(bf16[128,896]{1,0:T(8,128)(2,1)} %param.5) | copy-start | bytes 688132
  7.2 9.2 %copy-start.4 = (f32[128,8]{0,1:T(8,128)S(1)}, f32[128,8]{0,1:T(8,128)}, u32[]{:S(2)}) copy-start(f32[128,8]{0,1:T(8,128)} %param.7) | copy-start | bytes 12292
  7.2 9.2 %copy-start.3 = (bf16[128,8,256]{2,1,0:T(8,128)(2,1)S(1)}, bf16[128,8,256]{2,1,0:T(8,128)(2,1)}, u32[]{:S(2)}) copy-start(bf16[128,8,256]{2,1,0:T(8,128)(2,1)} %param.8) | copy-start | bytes 1572868
  7.2 175.9 %all-gather.5.cloned.1.call-start = ((), (), s32[]{:S(2)}) async-start(), calls=%async_computation.5 | async-start | bytes 6881280 | tf_op jit(solution)/shard_map/all_gather | solution.py:52
  109.1 136.7 %all-gather.7.cloned.1.call-start = ((), (), s32[]{:S(2)}) async-start(), calls=%async_computation.6 | async-start | bytes 6881280 | tf_op jit(solution)/shard_map/all_gather | solution.py:52
  182.8 133.2 %reduce-scatter.2.cloned.1.call-start = ((), (), s32[]{:S(2)}) async-start(), calls=%async_computation.4 | async-start | bytes 2752512 | tf_op jit(solution)/shard_map/reduce_scatter | solution.py:62
  253.6 1.5 copy-start.1
  256.6 5.0 %copy-start.2 = (bf16[256,4,896]{2,1,0:T(4,128)(2,1)S(1)}, bf16[256,4,896]{2,1,0:T(4,128)(2,1)}, u32[]{:S(2)}) copy-start(bf16[256,4,896]{2,1,0:T(4,128)(2,1)} %reshape_squeeze.3) | copy-start | bytes 5505028
Sparse Core Ops, SparseCore 0:
  109.2 63.3 all-gather.4
  182.9 62.7 all-gather.6
  253.7 18.2 reduce-scatter.1

commit v3 on v1

--- a/solution.py
+++ b/solution.py
@@ -41,17 +41,24 @@
     send = jnp.concatenate([send_grad, send_scaled], axis=1).reshape(
         experts, capacity, d_slice + hidden_slice
     )
+    section = lax.axis_index("section")
+    w_full = lax.all_gather(w_down[0], "section", axis=0, tiled=True)
+    w_slice = lax.dynamic_slice_in_dim(w_full, section * d_slice, d_slice, axis=1)
     recv = lax.all_to_all(send, "expert", split_axis=0, concat_axis=0, tiled=True)
     recv = recv.reshape(slot_count, d_slice + hidden_slice)
     recv_grad = recv[:, :d_slice]
     recv_scaled = recv[:, d_slice:]
-    spread = jnp.broadcast_to(recv_grad[None], (n_section, slot_count, d_slice))
-    gathered = lax.all_to_all(spread, "section", split_axis=0, concat_axis=0, tiled=True)
-    w_local = w_down[0].reshape(hidden_slice, n_section, d_slice)
-    unscaled = jnp.einsum("srd,hsd->rh", gathered, w_local, preferred_element_type=jnp.float32)
-    weight_part = jnp.einsum(
-        "rh,srd->hsd", recv_scaled, gathered, preferred_element_type=jnp.float32
-    ).astype(jnp.bfloat16).reshape(1, hidden_slice, n_section * d_slice)
+    scaled_all = lax.all_gather(recv_scaled, "section", axis=0, tiled=False)
+    partial = jnp.einsum("rd,hd->rh", recv_grad, w_slice, preferred_element_type=jnp.float32)
+    partial = partial.reshape(slot_count, n_section, hidden_slice)
+    partial = jnp.transpose(partial, (1, 0, 2))
+    pieces = lax.all_to_all(partial, "section", split_axis=0, concat_axis=0, tiled=True)
+    unscaled = jnp.sum(pieces, axis=0)
+    block = jnp.einsum(
+        "srh,rd->shd", scaled_all, recv_grad, preferred_element_type=jnp.float32
+    ).astype(jnp.bfloat16)
+    blocks = lax.all_to_all(block, "section", split_axis=0, concat_axis=0, tiled=True)
+    weight_part = jnp.transpose(blocks, (1, 0, 2)).reshape(1, hidden_slice, n_section * d_slice)
     grad_w = lax.psum_scatter(weight_part, "dp", scatter_dimension=2, tiled=True)
     returning = unscaled.astype(jnp.bfloat16).reshape(experts, capacity, hidden_slice)
     returned = lax.all_to_all(returning, "expert", split_axis=0, concat_axis=0, tiled=True)
@@ -75,6 +82,7 @@
         P(("dp", "expert"), None, "section"),
         P("expert", "section", None),
     )
+
     return jax.shard_map(
         local,
         mesh=mesh,

time: 340 us -> 419 us (1.23)
  waiting for transfers between devices: 0.02 us -> 223 us
  blocking collectives: 272 us -> 109 us
  starting transfers between devices: 0.04 us -> 22.5 us
  local copies, waits for them, and re-layouts: 25.7 us -> 15.6 us
  other arithmetic: 10 us -> 14.6 us
    all_to_all x2 -> x0, blocking collectives: 164 us -> none  [the longest x1 125 us: local(): lax.all_to_all(spread, 'section', split_axis=0, concat_axis=0, tiled=True)]
    all_gather x0 -> x2, waiting for transfers between devices: none -> 131 us  [the longest x1 82.5 us: local(): w_full = lax.all_gather(w_down[0], 'section', axis=0, tiled=True)]
    all_to_all x0 -> x3, waiting for transfers between devices: none -> 91.2 us  [the longest x1 69.2 us: local(): lax.all_to_all(partial, 'section', split_axis=0, concat_axis=0, tiled=True)]
    all_to_all x0 -> x3, starting transfers between devices: none -> 22.4 us  [the longest x1 13.4 us: local(): lax.all_to_all(returning, 'expert', split_axis=0, concat_axis=0, tiled=True)]
    broadcast_in_dim x1 -> x0, local copies, waits for them, and re-layouts: 4.98 us -> none  [local(): spread = jnp.broadcast_to(recv_grad[None], (n_section, slot_count, d_slice))]
    unnamed x14 -> x10, local copies, waits for them, and re-layouts: 9.35 us -> 5.08 us
  transfers between devices with their start and end apart: 1 -> 6, of which waited for: 0 -> 4; matrix products, arithmetic and copies ran while one was open for 3% -> 6% of each run, Pallas kernels for 0% -> 0%
where the time goes in v3:
time: 419 us; the launch traced here: 418 us
  waiting for transfers between devices  223 us (53%)
  blocking collectives  109 us (26%)
  starting transfers between devices  22.5 us (5%)
  matrix products  20 us (5%)
  local copies, waits for them, and re-layouts  15.6 us (4%)
  other arithmetic  14.6 us (3%)
  between operations  13.9 us (3%)
    all_to_all x1, blocking collectives, local(): lax.all_to_all(send, 'expert', split_axis=0, concat_axis=0, tiled=True)  99 us
    all_gather x1, waiting for transfers between devices, local(): w_full = lax.all_gather(w_down[0], 'section', axis=0, tiled=True)  82.5 us
    all_to_all x1, waiting for transfers between devices, local(): lax.all_to_all(partial, 'section', split_axis=0, concat_axis=0, tiled=True)  69.2 us
    all_gather x1, waiting for transfers between devices, local(): scaled_all = lax.all_gather(recv_scaled, 'section', axis=0, tiled=False)  48.7 us
    all_to_all x1, waiting for transfers between devices, local(): lax.all_to_all(returning, 'expert', split_axis=0, concat_axis=0, tiled=True)  21.9 us
    all_to_all x1, starting transfers between devices, local(): lax.all_to_all(returning, 'expert', split_axis=0, concat_axis=0, tiled=True)  13.4 us
    psum x1, blocking collectives, local(): grad_gates = lax.psum(gate_share, 'section')  9.49 us
    dot_general x1, matrix products, local(): jnp.einsum('rd,hd->rh', recv_grad, w_slice, preferred_element_type=jnp.fl...  8.47 us
  transfers between devices with their start and end apart: 6, of which 4 were waited for; matrix products, arithmetic and copies ran while one was open for 6% of the time, Pallas kernels for 0%

profile of v3, /device:TPU:16, one launch (start us, length us, event | category | flops | bytes accessed | tf_op | source)
XLA Modules:
  0.0 418.1 jit_solution(13954072477528761265)
XLA Ops:
  7.2 0.8 fusion.22
  8.0 0.1 fusion.23
  8.1 0.7 select_reduce_fusion
  8.9 0.7 convert_add_fusion
  9.6 0.1 copy.50
  9.7 5.6 %fusion.3 = pred[1536,128]{1,0:T(8,128)(4,1)S(1)} fusion(s32[128,8]{0,1:T(8,128)S(1)} %convert_add_fusion), kind=kLoop, calls=%fused_computation.5 | loop fusion | flops 2949120 | bytes 200704 | tf_op jit(solution)/shard_map/reduce_or | solution.py:18
  15.3 0.1 eq.70
  15.4 1.3 fusion.18
  16.6 1.6 fusion.9
  18.2 0.9 convolution_convert_fusion
  19.2 2.0 pad_maximum_fusion
  21.2 5.8 %copy.53 = bf16[1536,1152]{1,0:T(8,128)(2,1)} copy(bf16[1536,1152]{0,1:T(8,128)(2,1)} %pad_maximum_fusion) | data formatting | bytes 7077888 | tf_op jit(solution)/shard_map/concatenate | solution.py:41
  27.0 99.0 %all_to_all.20 = bf16[64,24,1152]{2,1,0:T(8,128)(2,1)S(1)} all-to-all(bf16[64,24,1152]{2,1,0:T(8,128)(2,1)} %bitcast.33), channel_id=1, replica_groups=mesh['dp'=2,'section'=4,'expert'=64] {'expert'}, dimensions={0} | all-to-all | bytes 7077888 | tf_op jit(solution)/shard_map/all_to_all | solution.py:47
  126.0 1.8 copy-done.1
  127.7 0.9 slice.9
  128.7 0.7 all-gather.5.cloned.1.call-update
  129.4 48.7 %all-gather.7.cloned.1.call-done = bf16[6144,256]{1,0:T(8,128)(2,1)} async-done(((bf16[1536,256]{1,0:T(8,128)(2,1)}), bf16[6144,256]{1,0:T(8,128)(2,1)}) %all-gather.7.cloned.1.call-update) | async-done | bytes 3145744 | tf_op jit(solution)/shard_map/all_gather | solution.py:51
  178.1 7.5 %fusion.15 = bf16[4,256,896]{2,1,0:T(8,128)(2,1)} fusion(bf16[4,1536,256]{2,1,0:T(8,128)(2,1)} %bitcast.41, bf16[1536,1152]{1,0:T(8,128)(2,1)} %bitcast.38), kind=kOutput, calls=%fused_computation.19 | convolution fusion | flops 2819489792 | bytes 7733248 | tf_op jit(solution)/shard_map/srh,rd->shd/dot_general | solution.py:57
  185.6 3.8 all-to-all-start.3
  189.4 82.5 %all-gather.5.cloned.1.call-done = bf16[1,1024,3584]{2,1,0:T(8,128)(2,1)} async-done(((bf16[1,256,3584]{2,1,0:T(8,128)(2,1)}), bf16[1,1024,3584]{2,1,0:T(8,128)(2,1)}) %all-gather.5.cloned.1.call-update) | async-done | bytes 7340048 | tf_op jit(solution)/shard_map/all_gather | solution.py:45
  271.8 8.5 %fusion.11 = f32[1536,1024]{0,1:T(8,128)} fusion(bf16[1536,1152]{1,0:T(8,128)(2,1)} %bitcast.39, bf16[1,1024,3584]{2,1,0:T(8,128)(2,1)} %all-gather.5.cloned.1.call-done, s32[]{:T(128)S(6)} %select_n.8), kind=kOutput, calls=%fused_computation.15 | convolution fusion | flops 2818572288 | bytes 10878980 | tf_op jit(solution)/shard_map/rd,hd->rh/dot_general | solution.py:52
  280.3 5.2 %all-to-all-start.1 = ((f32[4,1536,256]{1,2,0:T(8,128)}), f32[4,1536,256]{1,2,0:T(8,128)}, u32[]{:S(2)}, u32[]{:S(2)}) async-start(f32[4,1536,256]{1,2,0:T(8,128)} %bitcast.36), calls=%async_computation.1 | async-start | bytes 12582912 | tf_op jit(solution)/shard_map/all_to_all | solution.py:55
  285.6 2.4 copy.56
  288.1 69.2 %all-to-all-done.1 = f32[4,1536,256]{1,2,0:T(8,128)} async-done(((f32[4,1536,256]{1,2,0:T(8,128)}), f32[4,1536,256]{1,2,0:T(8,128)}, u32[]{:S(2)}, u32[]{:S(2)}) %all-to-all-start.1) | async-done | bytes 6291488 | tf_op jit(solution)/shard_map/all_to_all | solution.py:55
  357.3 3.5 reduce_sum.28
  360.9 1.2 copy.54
  362.0 13.4 %all-to-all-start.2 = ((bf16[64,24,256]{2,1,0:T(8,128)(2,1)}), bf16[64,24,256]{2,1,0:T(8,128)(2,1)S(1)}, u32[]{:S(2)}, u32[]{:S(2)}) async-start(bf16[64,24,256]{2,1,0:T(8,128)(2,1)} %bitcast.7), calls=%async_computation.2 | async-start | bytes 1572864 | tf_op jit(solution)/shard_map/all_to_all | solution.py:64
  375.4 2.2 copy.58
  377.6 21.9 %all-to-all-done.2 = bf16[64,24,256]{2,1,0:T(8,128)(2,1)S(1)} async-done(((bf16[64,24,256]{2,1,0:T(8,128)(2,1)}), bf16[64,24,256]{2,1,0:T(8,128)(2,1)S(1)}, u32[]{:S(2)}, u32[]{:S(2)}) %all-to-all-start.2) | async-done | bytes 786464 | tf_op jit(solution)/shard_map/all_to_all | solution.py:64
  399.6 1.4 fusion.19
  401.0 9.5 %psum.7 = f32[128,8]{0,1:T(8,128)} all-reduce(f32[128,8]{0,1:T(8,128)S(1)} %get-tuple-element.18), channel_id=1, replica_groups=mesh['dp'=2,'section'=4,'expert'=64] {'section'}, use_global_device_ids=true, to_apply=%region_5.6 | all-reduce | flops 1024 | bytes 8192 | tf_op jit(solution)/shard_map/psum | solution.py:73
  410.4 1.1 copy.57
  (14 shorter events, 0.2 us)
Async XLA Ops:
  7.2 11.1 %copy-start = (bf16[128,896]{1,0:T(8,128)(2,1)S(1)}, bf16[128,896]{1,0:T(8,128)(2,1)}, u32[]{:S(2)}) copy-start(bf16[128,896]{1,0:T(8,128)(2,1)} %param.5) | copy-start | bytes 688132
  7.2 170.9 %all-gather.7.cloned.1.call-start = ((), (), s32[]{:S(2)}) async-start(), calls=%async_computation.7 | async-start | bytes 3932160 | tf_op jit(solution)/shard_map/all_gather | solution.py:51
  126.0 1.8 copy-start.1
  128.7 143.1 %all-gather.5.cloned.1.call-start = ((), (), s32[]{:S(2)}) async-start(), calls=%async_computation.6 | async-start | bytes 9175040 | tf_op jit(solution)/shard_map/all_gather | solution.py:45
  185.6 94.7 %all-to-all-start.3 = ((bf16[4,256,896]{2,1,0:T(8,128)(2,1)}), bf16[4,256,896]{2,1,0:T(8,128)(2,1)S(1)}, u32[]{:S(2)}, u32[]{:S(2)}) async-start(bf16[4,256,896]{2,1,0:T(8,128)(2,1)} %fusion.15), calls=%async_computation.3 | async-start | bytes 3670016 | tf_op jit(solution)/shard_map/all_to_all | solution.py:60
  280.3 77.0 %all-to-all-start.1 = ((f32[4,1536,256]{1,2,0:T(8,128)}), f32[4,1536,256]{1,2,0:T(8,128)}, u32[]{:S(2)}, u32[]{:S(2)}) async-start(f32[4,1536,256]{1,2,0:T(8,128)} %bitcast.36), calls=%async_computation.1 | async-start | bytes 12582912 | tf_op jit(solution)/shard_map/all_to_all | solution.py:55
  285.6 89.8 %reduce-scatter.2.cloned.1.call-start = ((), (), s32[]{:S(2)}) async-start(), calls=%async_computation.5 | async-start | bytes 2752512 | tf_op jit(solution)/shard_map/reduce_scatter | solution.py:62
  360.8 38.7 %copy-start.2 = (bf16[128,8,256]{2,1,0:T(8,128)(2,1)S(1)}, bf16[128,8,256]{2,1,0:T(8,128)(2,1)}, u32[]{:S(2)}) copy-start(bf16[128,8,256]{2,1,0:T(8,128)(2,1)} %param.8) | copy-start | bytes 1572868
  360.8 38.7 %copy-start.3 = (f32[128,8]{0,1:T(8,128)S(1)}, f32[128,8]{0,1:T(8,128)}, u32[]{:S(2)}) copy-start(f32[128,8]{0,1:T(8,128)} %param.7) | copy-start | bytes 12292
  362.0 37.6 %all-to-all-start.2 = ((bf16[64,24,256]{2,1,0:T(8,128)(2,1)}), bf16[64,24,256]{2,1,0:T(8,128)(2,1)S(1)}, u32[]{:S(2)}, u32[]{:S(2)}) async-start(bf16[64,24,256]{2,1,0:T(8,128)(2,1)} %bitcast.7), calls=%async_computation.2 | async-start | bytes 1572864 | tf_op jit(solution)/shard_map/all_to_all | solution.py:64
Sparse Core Ops, SparseCore 0:
  128.8 49.2 all-gather.6
  180.2 91.5 all-gather.4
  289.2 19.4 reduce-scatter.1

commit v4 on v2

--- a/solution.py
+++ b/solution.py
@@ -15,8 +15,11 @@
     position = expert_ids * capacity + order_in
     slots = jnp.arange(experts * capacity, dtype=jnp.int32)
     sel_pairs = position.reshape(tok_count * top_count)[None, :] == slots[:, None]
-    sel_tok = jnp.any(position[None, :, :] == slots[:, None, None], axis=2)
-    return sel_pairs.astype(jnp.bfloat16), sel_tok.astype(jnp.bfloat16)
+    pairs = jnp.arange(tok_count * top_count, dtype=jnp.int32)
+    member = (pairs[:, None] // top_count == rows[None, :]).astype(jnp.bfloat16)
+    sel_pairs = sel_pairs.astype(jnp.bfloat16)
+    sel_tok = jnp.dot(sel_pairs, member, preferred_element_type=jnp.float32).astype(jnp.bfloat16)
+    return sel_pairs, sel_tok
 
 
 def local(grad_out, expert_ids, gate_weights, act, w_down):
@@ -42,25 +45,25 @@
         experts, capacity, d_slice + hidden_slice
     )
     w_local = w_down[0].reshape(hidden_slice, n_section, d_slice)
-    chunks = 2
-    step = capacity // chunks
-    received = []
-    for c in range(chunks):
-        part = lax.all_to_all(
-            send[:, c * step:(c + 1) * step], "expert", split_axis=0, concat_axis=0, tiled=True
-        ).reshape(experts * step, d_slice + hidden_slice)
-        gathered = lax.all_gather(part[:, :d_slice], "section", axis=0, tiled=False)
-        received.append((part[:, d_slice:], gathered))
+    recv = lax.all_to_all(send, "expert", split_axis=0, concat_axis=0, tiled=True)
+    recv = recv.reshape(slot_count, d_slice + hidden_slice)
+    half = slot_count // 2
+    first = recv[:half]
+    second = recv[half:]
+    gathered_first = lax.all_gather(first[:, :d_slice], "section", axis=0, tiled=False)
+    spread = jnp.broadcast_to(second[None, :, :d_slice], (n_section, slot_count - half, d_slice))
+    gathered_second = lax.all_to_all(spread, "section", split_axis=0, concat_axis=0, tiled=True)
+    received = [(first[:, d_slice:], gathered_first), (second[:, d_slice:], gathered_second)]
     weight_acc = None
     returning = []
     for recv_scaled, gathered in received:
         unscaled = jnp.einsum("srd,hsd->rh", gathered, w_local, preferred_element_type=jnp.float32)
-        returning.append(unscaled.astype(jnp.bfloat16).reshape(experts, step, hidden_slice))
+        returning.append(unscaled.astype(jnp.bfloat16))
         term = jnp.einsum("rh,srd->hsd", recv_scaled, gathered, preferred_element_type=jnp.float32)
         weight_acc = term if weight_acc is None else weight_acc + term
     weight_part = weight_acc.astype(jnp.bfloat16).reshape(1, hidden_slice, n_section * d_slice)
     grad_w = lax.psum_scatter(weight_part, "dp", scatter_dimension=2, tiled=True)
-    returning = jnp.concatenate(returning, axis=1)
+    returning = jnp.concatenate(returning, axis=0).reshape(experts, capacity, hidden_slice)
     returned = lax.all_to_all(returning, "expert", split_axis=0, concat_axis=0, tiled=True)
     unscaled_tok = lax.dot_general(
         sel_pairs,

time: 325 us -> 325 us (level)
  the two profiles are of different devices: /device:TPU:16 before, /device:TPU:18 now
where the time goes in v4:
time: 325 us
  blocking collectives  151 us (46%)
  waiting for transfers between devices  102 us (31%)
  matrix products  24.5 us (8%)
  local copies, waits for them, and re-layouts  20.8 us (6%)
  between operations  14.2 us (4%)
  other arithmetic  6.64 us (2%)
  starting transfers between devices  5.67 us (2%)
    all_gather x1, waiting for transfers between devices, local(): lax.all_gather(first[:, :d_slice], 'section', axis=0, tiled=False)  102 us
    all_to_all x1, blocking collectives, local(): lax.all_to_all(send, 'expert', split_axis=0, concat_axis=0, tiled=True)  99.4 us
    all_to_all x1, blocking collectives, local(): lax.all_to_all(returning, 'expert', split_axis=0, concat_axis=0, tiled=True)  38.3 us
    psum x1, blocking collectives, local(): grad_gates = lax.psum(gate_share, 'section')  12.8 us
    dot_general x2, matrix products, local(): jnp.einsum('rh,srd->hsd', recv_scaled, gathered, preferred_element_type=j...  11.5 us
  transfers between devices with their start and end apart: 3, of which 1 were waited for; matrix products, arithmetic and copies ran while one was open for 6% of the time, Pallas kernels for 0%

profile of v4, /device:TPU:18, one launch (start us, length us, event | category | flops | bytes accessed | tf_op | source)
XLA Modules:
  0.0 324.6 jit_solution(13033326550447104199)
XLA Ops:
  7.2 0.0 all-gather.3.cloned.1.call-start
  7.2 0.8 fusion.33
  8.0 0.1 fusion.34
  8.1 0.7 select_reduce_fusion
  8.9 0.7 convert_add_fusion
  9.6 0.1 copy.29
  9.7 0.1 eq.67
  9.8 1.3 fusion.26
  11.1 2.5 fusion.8
  13.5 2.9 convolution_convert_fusion
  16.5 3.1 pad_maximum_fusion
  19.6 5.8 %copy.32 = bf16[1536,1152]{1,0:T(8,128)(2,1)} copy(bf16[1536,1152]{0,1:T(8,128)(2,1)} %pad_maximum_fusion) | data formatting | bytes 7077888 | tf_op jit(solution)/shard_map/concatenate | solution.py:44
  25.4 99.4 %all_to_all.15 = bf16[64,24,1152]{2,1,0:T(8,128)(2,1)S(1)} all-to-all(bf16[64,24,1152]{2,1,0:T(8,128)(2,1)} %bitcast.40), channel_id=1, replica_groups=mesh['dp'=2,'section'=4,'expert'=64] {'expert'}, dimensions={0} | all-to-all | bytes 7077888 | tf_op jit(solution)/shard_map/all_to_all | solution.py:48
  124.8 0.3 fusion.38
  125.1 1.3 copy-done.2
  126.3 1.2 slice.33
  127.5 0.1 slice.35
  127.7 2.8 broadcast_in_dim.16
  130.4 5.6 %all-to-all-start.1 = ((bf16[4,768,896]{2,1,0:T(8,128)(2,1)}), bf16[4,768,896]{2,1,0:T(8,128)(2,1)}, u32[]{:S(2)}, u32[]{:S(2)}) async-start(bf16[4,768,896]{2,1,0:T(8,128)(2,1)} %broadcast_in_dim.16), calls=%async_computation.1 | async-start | bytes 11010048 | tf_op jit(solution)/shard_map/all_to_all | solution.py:55
  136.1 102.4 %all-gather.3.cloned.1.call-done = bf16[3072,896]{1,0:T(8,128)(2,1)} async-done(((bf16[768,896]{1,0:T(8,128)(2,1)}), bf16[3072,896]{1,0:T(8,128)(2,1)}) %all-gather.3.cloned.1.call-update) | async-done | bytes 5505040 | tf_op jit(solution)/shard_map/all_gather | solution.py:53
  238.4 6.1 %fusion.30 = f32[256,4,896]{2,0,1:T(8,128)} fusion(bf16[4,768,896]{2,1,0:T(8,128)(2,1)} %bitcast.46, bf16[768,1152]{1,0:T(8,128)(2,1)} %bitcast.45), kind=kOutput, calls=%fused_computation.33 | convolution fusion | flops 1409286144 | bytes 9568256 | tf_op jit(solution)/shard_map/rh,srd->hsd/dot_general | solution.py:62
  244.6 5.4 %add_convert_fusion = bf16[256,4,896]{2,0,1:T(8,128)(2,1)S(1)} fusion(f32[256,4,896]{2,0,1:T(8,128)} %fusion.30, bf16[4,768,896]{2,1,0:T(8,128)(2,1)} %all-to-all-done.1, bf16[768,1152]{1,0:T(8,128)(2,1)} %bitcast.43), kind=kOutput, calls=%fused_computation.6 | convolution fusion | flops 1411121152 | bytes 11403264 | tf_op jit(solution)/shard_map/rh,srd->hsd/dot_general | solution.py:62
  250.0 2.4 copy.37
  252.4 3.4 %reshape_squeeze.3 = bf16[256,4,896]{2,1,0:T(4,128)(2,1)S(1)} reshape(bf16[1,256,3584]{2,1,0:T(8,128)(2,1)} %param.9) | data formatting | bytes 3670016 | tf_op jit(solution)/shard_map/reshape;squeeze | solution.py:47
  255.9 4.3 %fusion.20 = bf16[768,256]{1,0:T(8,128)(2,1)S(1)} fusion(bf16[4,768,896]{2,1,0:T(8,128)(2,1)} %all-to-all-done.1, bf16[256,4,896]{2,1,0:T(4,128)(2,1)S(1)} %reshape_squeeze.3), kind=kOutput, calls=%fused_computation.22 | convolution fusion | flops 1409482752 | bytes 7733248 | tf_op jit(solution)/shard_map/srd,hsd->rh/dot_general | solution.py:60
  260.3 1.6 fusion.23
  261.9 0.1 pad_maximum_fusion.1
  262.0 38.3 %all_to_all.16 = bf16[64,24,256]{2,1,0:T(8,128)(2,1)S(1)} all-to-all(bf16[64,24,256]{2,1,0:T(8,128)(2,1)S(1)} %bitcast.50), channel_id=1, replica_groups=mesh['dp'=2,'section'=4,'expert'=64] {'expert'}, dimensions={0} | all-to-all | bytes 1572864 | tf_op jit(solution)/shard_map/all_to_all | solution.py:67
  300.2 1.4 fusion.27
  301.6 1.1 copy.38
  302.7 12.8 %psum.7 = f32[128,8]{0,1:T(8,128)} all-reduce(f32[128,8]{0,1:T(8,128)S(1)} %get-tuple-element.14), channel_id=1, replica_groups=mesh['dp'=2,'section'=4,'expert'=64] {'section'}, use_global_device_ids=true, to_apply=%region_3.4 | all-reduce | flops 1024 | bytes 8192 | tf_op jit(solution)/shard_map/psum | solution.py:76
  315.6 2.2 copy.39
  (20 shorter events, 0.1 us)
Async XLA Ops:
  7.2 6.4 %copy-start = (bf16[128,896]{1,0:T(8,128)(2,1)S(1)}, bf16[128,896]{1,0:T(8,128)(2,1)}, u32[]{:S(2)}) copy-start(bf16[128,896]{1,0:T(8,128)(2,1)} %param.5) | copy-start | bytes 688132
  7.2 231.2 %all-gather.3.cloned.1.call-start = ((), (), s32[]{:S(2)}) async-start(), calls=%async_computation.5 | async-start | bytes 6881280 | tf_op jit(solution)/shard_map/all_gather | solution.py:53
  125.0 1.3 copy-start.2
  125.1 5.4 %copy-start.1 = (bf16[32,24,1152]{2,1,0:T(8,128)(2,1)}, bf16[32,24,1152]{2,1,0:T(8,128)(2,1)S(1)}, u32[]{:S(2)}) copy-start(bf16[32,24,1152]{2,1,0:T(8,128)(2,1)S(1)} %get-tuple-element.13) | copy-start | bytes 5308420
  130.4 114.1 %all-to-all-start.1 = ((bf16[4,768,896]{2,1,0:T(8,128)(2,1)}), bf16[4,768,896]{2,1,0:T(8,128)(2,1)}, u32[]{:S(2)}, u32[]{:S(2)}) async-start(bf16[4,768,896]{2,1,0:T(8,128)(2,1)} %broadcast_in_dim.16), calls=%async_computation.1 | async-start | bytes 11010048 | tf_op jit(solution)/shard_map/all_to_all | solution.py:55
  136.1 179.5 %reduce-scatter.2.cloned.1.call-start = ((), (), s32[]{:S(2)}) async-start(), calls=%async_computation.4 | async-start | bytes 2752512 | tf_op jit(solution)/shard_map/reduce_scatter | solution.py:65
  252.4 7.8 %slice-start = ((s8[5505024]{0:T(1024)(128)(4,1)}), s8[1310720]{0:T(1024)(128)(4,1)S(1)}, s32[]{:S(2)}) async-start(s8[5505024]{0:T(1024)(128)(4,1)} %bitcast.47), calls=%async_computation.6 | async-start | bytes 2621440
  255.9 4.4 %slice-start.1 = ((s8[5505024]{0:T(1024)(128)(4,1)}), s8[4194304]{0:T(1024)(128)(4,1)S(1)}, s32[]{:S(2)}) async-start(s8[5505024]{0:T(1024)(128)(4,1)} %bitcast.47), calls=%async_computation.7 | async-start | bytes 8388608
  260.2 40.0 %copy-start.3 = (bf16[128,8,256]{2,1,0:T(8,128)(2,1)S(1)}, bf16[128,8,256]{2,1,0:T(8,128)(2,1)}, u32[]{:S(2)}) copy-start(bf16[128,8,256]{2,1,0:T(8,128)(2,1)} %param.8) | copy-start | bytes 1572868
  260.3 40.0 %copy-start.4 = (f32[128,8]{0,1:T(8,128)S(1)}, f32[128,8]{0,1:T(8,128)}, u32[]{:S(2)}) copy-start(f32[128,8]{0,1:T(8,128)} %param.7) | copy-start | bytes 12292
Sparse Core Ops, SparseCore 0:
  127.7 110.7 all-gather.2
  252.6 22.7 reduce-scatter.1

commit v5 on v2

--- a/solution.py
+++ b/solution.py
@@ -15,8 +15,11 @@
     position = expert_ids * capacity + order_in
     slots = jnp.arange(experts * capacity, dtype=jnp.int32)
     sel_pairs = position.reshape(tok_count * top_count)[None, :] == slots[:, None]
-    sel_tok = jnp.any(position[None, :, :] == slots[:, None, None], axis=2)
-    return sel_pairs.astype(jnp.bfloat16), sel_tok.astype(jnp.bfloat16)
+    pairs = jnp.arange(tok_count * top_count, dtype=jnp.int32)
+    member = (pairs[:, None] // top_count == rows[None, :]).astype(jnp.bfloat16)
+    sel_pairs = sel_pairs.astype(jnp.bfloat16)
+    sel_tok = jnp.dot(sel_pairs, member, preferred_element_type=jnp.float32).astype(jnp.bfloat16)
+    return sel_pairs, sel_tok
 
 
 def local(grad_out, expert_ids, gate_weights, act, w_down):
@@ -82,6 +85,7 @@
         P(("dp", "expert"), None, "section"),
         P("expert", "section", None),
     )
+
     return jax.shard_map(
         local,
         mesh=mesh,

time: 325 us -> 325 us (level)
  other arithmetic: 10.3 us -> 6.9 us
    reduce_or x1 -> x0, other arithmetic: 5.56 us -> none  [routing(): sel_tok = jnp.any(position[None, :, :] == slots[:, None, None], axis=2)]
where the time goes in v5:
time: 325 us; the launch traced here: 324 us
  blocking collectives  191 us (59%)
  waiting for transfers between devices  56.6 us (17%)
  matrix products  27.7 us (9%)
  local copies, waits for them, and re-layouts  27.5 us (8%)
  between operations  13.9 us (4%)
  other arithmetic  6.9 us (2%)
    all_to_all x2, blocking collectives, local(): lax.all_to_all(send[:, c * step:(c + 1) * step], 'expert', split_axis=0,...  144 us
    all_gather x2, waiting for transfers between devices, local(): gathered = lax.all_gather(part[:, :d_slice], 'section', axis=0, tiled=False)  56.5 us
    all_to_all x1, blocking collectives, local(): lax.all_to_all(returning, 'expert', split_axis=0, concat_axis=0, tiled=True)  37.8 us
    dot_general x2, matrix products, local(): jnp.einsum('rh,srd->hsd', recv_scaled, gathered, preferred_element_type=j...  11.6 us
    psum x1, blocking collectives, local(): grad_gates = lax.psum(gate_share, 'section')  9.63 us
    dot_general x2, matrix products, local(): jnp.einsum('srd,hsd->rh', gathered, w_local, preferred_element_type=jnp.f...  9.06 us
  transfers between devices with their start and end apart: 3, of which 1 were waited for; matrix products, arithmetic and copies ran while one was open for 7% of the time, Pallas kernels for 0%

profile of v5, /device:TPU:16, one launch (start us, length us, event | category | flops | bytes accessed | tf_op | source)
XLA Modules:
  0.0 324.3 jit_solution(8274617675386091764)
XLA Ops:
  7.2 0.8 fusion.33
  8.0 0.1 fusion.34
  8.1 0.7 select_reduce_fusion
  8.9 0.7 convert_add_fusion
  9.6 0.1 copy.29
  9.8 1.3 fusion.26
  11.1 2.5 fusion.8
  13.5 2.9 convolution_convert_fusion
  16.5 3.2 pad_maximum_fusion
  19.7 5.8 %copy.32 = bf16[1536,1152]{1,0:T(8,128)(2,1)} copy(bf16[1536,1152]{0,1:T(8,128)(2,1)} %pad_maximum_fusion) | data formatting | bytes 7077888 | tf_op jit(solution)/shard_map/concatenate | solution.py:44
  25.5 4.7 %fusion.38 = (bf16[64,12,1152]{2,1,0:T(8,128)(2,1)S(1)}, bf16[64,12,1152]{2,1,0:T(8,128)(2,1)}) fusion(bf16[64,24,1152]{2,1,0:T(8,128)(2,1)} %bitcast.38), kind=kLoop, calls=%fused_computation.48 | loop fusion | bytes 7077888 | tf_op jit(solution)/shard_map/slice | solution.py:53
  30.2 74.4 %all_to_all.15 = bf16[64,12,1152]{2,1,0:T(8,128)(2,1)S(1)} all-to-all(bf16[64,12,1152]{2,1,0:T(8,128)(2,1)S(1)} %get-tuple-element.12), channel_id=1, replica_groups=mesh['dp'=2,'section'=4,'expert'=64] {'expert'}, dimensions={0} | all-to-all | bytes 3538944 | tf_op jit(solution)/shard_map/all_to_all | solution.py:52
  104.6 1.4 reshape.90
  106.0 2.5 slice.25
  108.6 69.6 %all_to_all.16 = bf16[64,12,1152]{2,1,0:T(8,128)(2,1)S(1)} all-to-all(bf16[64,12,1152]{2,1,0:T(8,128)(2,1)} %get-tuple-element.13), channel_id=1, replica_groups=mesh['dp'=2,'section'=4,'expert'=64] {'expert'}, dimensions={0} | all-to-all | bytes 3538944 | tf_op jit(solution)/shard_map/all_to_all | solution.py:52
  178.3 1.4 reshape.92
  179.7 2.5 slice.27
  182.3 0.2 reduce-scatter.2.cloned.1.call-start
  182.5 6.2 %fusion.30 = f32[256,4,896]{2,0,1:T(8,128)} fusion(bf16[4,768,896]{2,1,0:T(8,128)(2,1)} %bitcast.40, bf16[768,1152]{1,0:T(8,128)(2,1)} %reshape.90), kind=kOutput, calls=%fused_computation.33 | convolution fusion | flops 1409286144 | bytes 9568256 | tf_op jit(solution)/shard_map/rh,srd->hsd/dot_general | solution.py:62
  188.7 56.5 %all-gather.7.cloned.1.call-done = bf16[3072,896]{1,0:T(8,128)(2,1)} async-done(((bf16[768,896]{1,0:T(8,128)(2,1)}), bf16[3072,896]{1,0:T(8,128)(2,1)}) %all-gather.7.cloned.1.call-update) | async-done | bytes 5505040 | tf_op jit(solution)/shard_map/all_gather | solution.py:55
  245.2 5.4 %add_convert_fusion = bf16[256,4,896]{2,0,1:T(8,128)(2,1)S(1)} fusion(f32[256,4,896]{2,0,1:T(8,128)} %fusion.30, bf16[4,768,896]{2,1,0:T(8,128)(2,1)} %bitcast.42, bf16[768,1152]{1,0:T(8,128)(2,1)} %reshape.92), kind=kOutput, calls=%fused_computation.6 | convolution fusion | flops 1411121152 | bytes 11403264 | tf_op jit(solution)/shard_map/rh,srd->hsd/dot_general | solution.py:62
  250.7 2.4 copy.37
  253.1 1.5 copy-done.1
  254.6 1.5 reshape_squeeze.3
  256.1 4.9 %fusion.23 = bf16[768,256]{1,0:T(8,128)(2,1)S(1)} fusion(bf16[4,768,896]{2,1,0:T(8,128)(2,1)} %bitcast.41, bf16[256,4,896]{2,1,0:T(4,128)(2,1)} %reshape_squeeze.3), kind=kOutput, calls=%fused_computation.23 | convolution fusion | flops 1409482752 | bytes 7733248 | tf_op jit(solution)/shard_map/srd,hsd->rh/dot_general | solution.py:60
  261.1 4.2 %fusion.20 = bf16[768,256]{1,0:T(8,128)(2,1)S(1)} fusion(bf16[4,768,896]{2,1,0:T(8,128)(2,1)} %bitcast.43, bf16[256,4,896]{2,1,0:T(4,128)(2,1)S(1)} %copy-done.2), kind=kOutput, calls=%fused_computation.22 | convolution fusion | flops 1409482752 | bytes 7733248 | tf_op jit(solution)/shard_map/srd,hsd->rh/dot_general | solution.py:60
  265.4 0.3 pad_maximum_fusion.1
  265.6 37.8 %all_to_all.17 = bf16[64,24,256]{2,1,0:T(8,128)(2,1)S(1)} all-to-all(bf16[64,24,256]{2,1,0:T(8,128)(2,1)S(1)} %pad_maximum_fusion.1), channel_id=1, replica_groups=mesh['dp'=2,'section'=4,'expert'=64] {'expert'}, dimensions={0} | all-to-all | bytes 1572864 | tf_op jit(solution)/shard_map/all_to_all | solution.py:67
  303.5 1.4 fusion.27
  304.9 1.1 copy.38
  305.9 9.6 %psum.7 = f32[128,8]{0,1:T(8,128)} all-reduce(f32[128,8]{0,1:T(8,128)S(1)} %get-tuple-element.14), channel_id=1, replica_groups=mesh['dp'=2,'section'=4,'expert'=64] {'section'}, use_global_device_ids=true, to_apply=%region_3.4 | all-reduce | flops 1024 | bytes 8192 | tf_op jit(solution)/shard_map/psum | solution.py:76
  315.6 2.2 copy.39
  (20 shorter events, 0.5 us)
Async XLA Ops:
  7.2 6.4 %copy-start = (bf16[128,896]{1,0:T(8,128)(2,1)S(1)}, bf16[128,896]{1,0:T(8,128)(2,1)}, u32[]{:S(2)}) copy-start(bf16[128,896]{1,0:T(8,128)(2,1)} %param.5) | copy-start | bytes 688132
  7.2 175.3 %all-gather.5.cloned.1.call-start = ((), (), s32[]{:S(2)}) async-start(), calls=%async_computation.5 | async-start | bytes 6881280 | tf_op jit(solution)/shard_map/all_gather | solution.py:55
  108.6 136.6 %all-gather.7.cloned.1.call-start = ((), (), s32[]{:S(2)}) async-start(), calls=%async_computation.6 | async-start | bytes 6881280 | tf_op jit(solution)/shard_map/all_gather | solution.py:55
  182.3 133.3 %reduce-scatter.2.cloned.1.call-start = ((), (), s32[]{:S(2)}) async-start(), calls=%async_computation.4 | async-start | bytes 2752512 | tf_op jit(solution)/shard_map/reduce_scatter | solution.py:65
  253.1 1.5 copy-start.1
  256.1 5.0 %copy-start.2 = (bf16[256,4,896]{2,1,0:T(4,128)(2,1)S(1)}, bf16[256,4,896]{2,1,0:T(4,128)(2,1)}, u32[]{:S(2)}) copy-start(bf16[256,4,896]{2,1,0:T(4,128)(2,1)} %reshape_squeeze.3) | copy-start | bytes 5505028
  265.3 38.2 %copy-start.3 = (bf16[128,8,256]{2,1,0:T(8,128)(2,1)S(1)}, bf16[128,8,256]{2,1,0:T(8,128)(2,1)}, u32[]{:S(2)}) copy-start(bf16[128,8,256]{2,1,0:T(8,128)(2,1)} %param.8) | copy-start | bytes 1572868
  265.3 38.2 %copy-start.4 = (f32[128,8]{0,1:T(8,128)S(1)}, f32[128,8]{0,1:T(8,128)}, u32[]{:S(2)}) copy-start(f32[128,8]{0,1:T(8,128)} %param.7) | copy-start | bytes 12292
Sparse Core Ops, SparseCore 0:
  108.7 63.3 all-gather.4
  182.4 62.8 all-gather.6
  253.3 18.2 reduce-scatter.1

commit v6 on v2

--- a/solution.py
+++ b/solution.py
@@ -15,8 +15,8 @@
     position = expert_ids * capacity + order_in
     slots = jnp.arange(experts * capacity, dtype=jnp.int32)
     sel_pairs = position.reshape(tok_count * top_count)[None, :] == slots[:, None]
-    sel_tok = jnp.any(position[None, :, :] == slots[:, None, None], axis=2)
-    return sel_pairs.astype(jnp.bfloat16), sel_tok.astype(jnp.bfloat16)
+    sel_pairs = sel_pairs.astype(jnp.bfloat16)
+    return sel_pairs, position
 
 
 def local(grad_out, expert_ids, gate_weights, act, w_down):
@@ -30,24 +30,31 @@
     pair_count = tok_count * top_count
     slot_count = experts * capacity
 
-    sel_pairs, sel_tok = routing(expert_ids, experts, capacity)
+    sel_pairs, position = routing(expert_ids, experts, capacity)
     scaled = (
         (gate_weights[:, :, None] * act.astype(jnp.float32))
         .astype(jnp.bfloat16)
         .reshape(pair_count, hidden_slice)
     )
-    send_scaled = jnp.dot(sel_pairs, scaled, preferred_element_type=jnp.float32).astype(jnp.bfloat16)
-    send_grad = jnp.dot(sel_tok, grad_out, preferred_element_type=jnp.float32).astype(jnp.bfloat16)
-    send = jnp.concatenate([send_grad, send_scaled], axis=1).reshape(
-        experts, capacity, d_slice + hidden_slice
+    payload = jnp.concatenate(
+        [jnp.repeat(grad_out, top_count, axis=0), scaled], axis=1
     )
+    flat_pos = position.reshape(pair_count)
     w_local = w_down[0].reshape(hidden_slice, n_section, d_slice)
     chunks = 2
     step = capacity // chunks
     received = []
     for c in range(chunks):
+        chunk_slots = (
+            jnp.arange(experts, dtype=jnp.int32)[:, None] * capacity
+            + c * step
+            + jnp.arange(step, dtype=jnp.int32)[None, :]
+        ).reshape(experts * step)
+        sel_c = (flat_pos[None, :] == chunk_slots[:, None]).astype(jnp.bfloat16)
+        send_c = jnp.dot(sel_c, payload, preferred_element_type=jnp.float32).astype(jnp.bfloat16)
         part = lax.all_to_all(
-            send[:, c * step:(c + 1) * step], "expert", split_axis=0, concat_axis=0, tiled=True
+            send_c.reshape(experts, step, d_slice + hidden_slice),
+            "expert", split_axis=0, concat_axis=0, tiled=True,
         ).reshape(experts * step, d_slice + hidden_slice)
         gathered = lax.all_gather(part[:, :d_slice], "section", axis=0, tiled=False)
         received.append((part[:, d_slice:], gathered))
@@ -82,6 +89,7 @@
         P(("dp", "expert"), None, "section"),
         P("expert", "section", None),
     )
+
     return jax.shard_map(
         local,
         mesh=mesh,

time: 325 us -> 321 us (0.988)
  other arithmetic: 10.3 us -> 3.56 us
  matrix products: 24.8 us -> 30.8 us
  local copies, waits for them, and re-layouts: 27.5 us -> 23 us
    reshape x2 -> x5, local copies, waits for them, and re-layouts: 2.85 us -> 10.1 us  [the longest x2 5.08 us: local(): part = lax.all_to_all(send_c.reshape(experts, step, d_slice + hidden_slic...]
    dot_general x2, matrix products: 2.54 us -> 8.56 us  [local(): jnp.dot(sel_c, payload, preferred_element_type=jnp.float32)]
    concatenate x1 -> x0, local copies, waits for them, and re-layouts: 5.76 us -> none  [local(): jnp.concatenate([send_grad, send_scaled], axis=1)]
    reduce_or x1 -> x0, other arithmetic: 5.56 us -> none  [routing(): sel_tok = jnp.any(position[None, :, :] == slots[:, None, None], axis=2)]
    slice x1 -> x0, local copies, waits for them, and re-layouts: 4.71 us -> none  [local(): send[:, c * step:(c + 1) * step]]
  transfers between devices with their start and end apart: 3 -> 3, of which waited for: 1 -> 1; matrix products, arithmetic and copies ran while one was open for 7% -> 10% of each run, Pallas kernels for 0% -> 0%
where the time goes in v6:
time: 321 us; the launch traced here: 320 us
  blocking collectives  191 us (60%)
  waiting for transfers between devices  57.7 us (18%)
  matrix products  30.8 us (10%)
  local copies, waits for them, and re-layouts  23 us (7%)
  between operations  14 us (4%)
  other arithmetic  3.56 us (1%)
    all_to_all x2, blocking collectives, local(): lax.all_to_all(send_c.reshape(experts, step, d_slice + hidden_slice), 'ex...  143 us
    all_gather x2, waiting for transfers between devices, local(): gathered = lax.all_gather(part[:, :d_slice], 'section', axis=0, tiled=False)  57.7 us
    all_to_all x1, blocking collectives, local(): lax.all_to_all(returning, 'expert', split_axis=0, concat_axis=0, tiled=True)  37.8 us
    dot_general x2, matrix products, local(): jnp.einsum('rh,srd->hsd', recv_scaled, gathered, preferred_element_type=j...  11.6 us
    psum x1, blocking collectives, local(): grad_gates = lax.psum(gate_share, 'section')  9.62 us
    dot_general x2, matrix products, local(): jnp.einsum('srd,hsd->rh', gathered, w_local, preferred_element_type=jnp.f...  9.06 us
    dot_general x2, matrix products, local(): jnp.dot(sel_c, payload, preferred_element_type=jnp.float32)  8.56 us
  transfers between devices with their start and end apart: 3, of which 1 were waited for; matrix products, arithmetic and copies ran while one was open for 10% of the time, Pallas kernels for 0%

profile of v6, /device:TPU:16, one launch (start us, length us, event | category | flops | bytes accessed | tf_op | source)
XLA Modules:
  0.0 320.2 jit_solution(6322851284690109109)
XLA Ops:
  7.2 0.8 fusion.29
  8.2 0.7 select_reduce_fusion
  8.9 0.7 convert_add_fusion
  9.8 0.2 broadcast_bitcast_fusion
  10.1 0.9 fusion.26
  11.0 0.3 copy.57
  11.5 0.6 copy-done.7
  12.1 3.5 %convolution_convert_fusion.1 = bf16[768,1152]{1,0:T(8,128)(2,1)} fusion(s32[1024]{0:T(1024)S(1)} %eq.72, s32[768]{0:T(1024)S(1)} %add.65, bf16[1024,256]{1,0:T(8,128)(2,1)S(1)} %bitcast.44, bf16[1024,896]{1,0:T(8,128)(2,1)S(1)} %broadcast_bitcast_fusion), kind=kOutput, calls=%fused_computation.5 | convolution fusion | flops 1818329088 | bytes 4135936 | tf_op jit(solution)/shard_map/dot_general | solution.py:54
  15.6 2.4 reshape.95
  18.0 74.5 %all_to_all.15 = bf16[64,12,1152]{2,1,0:T(8,128)(2,1)} all-to-all(bf16[64,12,1152]{2,1,0:T(8,128)(2,1)S(1)} %reshape.95), channel_id=1, replica_groups=mesh['dp'=2,'section'=4,'expert'=64] {'expert'}, dimensions={0} | all-to-all | bytes 3538944 | tf_op jit(solution)/shard_map/all_to_all | solution.py:55
  92.5 2.5 reshape.96
  95.1 1.2 slice.16
  96.8 5.1 %convolution_convert_fusion = bf16[768,1152]{1,0:T(8,128)(2,1)} fusion(s32[1024]{0:T(1024)S(1)} %eq.72, s32[768]{0:T(1024)S(1)} %add.71, bf16[1024,256]{1,0:T(8,128)(2,1)S(1)} %bitcast.45, bf16[1024,896]{1,0:T(8,128)(2,1)} %copy-done.5), kind=kOutput, calls=%fused_computation.4 | convolution fusion | flops 1818329088 | bytes 4135936 | tf_op jit(solution)/shard_map/dot_general | solution.py:54
  101.8 2.4 reshape.98
  104.2 68.9 %all_to_all.16 = bf16[64,12,1152]{2,1,0:T(8,128)(2,1)} all-to-all(bf16[64,12,1152]{2,1,0:T(8,128)(2,1)S(1)} %reshape.98), channel_id=1, replica_groups=mesh['dp'=2,'section'=4,'expert'=64] {'expert'}, dimensions={0} | all-to-all | bytes 3538944 | tf_op jit(solution)/shard_map/all_to_all | solution.py:55
  173.2 2.5 reshape.99
  175.7 1.3 slice.17
  177.1 0.2 reduce-scatter.2.cloned.1.call-start
  177.3 6.2 %fusion.28 = f32[256,4,896]{2,0,1:T(8,128)} fusion(bf16[4,768,896]{2,1,0:T(8,128)(2,1)} %bitcast.39, bf16[768,1152]{1,0:T(8,128)(2,1)} %copy-done.1), kind=kOutput, calls=%fused_computation.32 | convolution fusion | flops 1409286144 | bytes 9568256 | tf_op jit(solution)/shard_map/rh,srd->hsd/dot_general | solution.py:66
  183.5 57.6 %all-gather.7.cloned.1.call-done = bf16[3072,896]{1,0:T(8,128)(2,1)} async-done(((bf16[768,896]{1,0:T(8,128)(2,1)}), bf16[3072,896]{1,0:T(8,128)(2,1)}) %all-gather.7.cloned.1.call-update) | async-done | bytes 5505040 | tf_op jit(solution)/shard_map/all_gather | solution.py:59
  241.2 5.4 %add_convert_fusion = bf16[256,4,896]{2,0,1:T(8,128)(2,1)S(1)} fusion(f32[256,4,896]{2,0,1:T(8,128)} %fusion.28, bf16[4,768,896]{2,1,0:T(8,128)(2,1)} %bitcast.41, bf16[768,1152]{1,0:T(8,128)(2,1)} %copy-done.2), kind=kOutput, calls=%fused_computation.3 | convolution fusion | flops 1411121152 | bytes 11403264 | tf_op jit(solution)/shard_map/rh,srd->hsd/dot_general | solution.py:66
  246.6 2.4 copy.37
  249.0 1.5 copy-done.3
  250.5 1.5 reshape_squeeze.3
  252.0 4.9 %fusion.20 = bf16[768,256]{1,0:T(8,128)(2,1)S(1)} fusion(bf16[4,768,896]{2,1,0:T(8,128)(2,1)} %bitcast.42, bf16[256,4,896]{2,1,0:T(4,128)(2,1)} %reshape_squeeze.3), kind=kOutput, calls=%fused_computation.22 | convolution fusion | flops 1409482752 | bytes 7733248 | tf_op jit(solution)/shard_map/srd,hsd->rh/dot_general | solution.py:64
  257.0 4.2 %fusion.23 = bf16[768,256]{1,0:T(8,128)(2,1)S(1)} fusion(bf16[4,768,896]{2,1,0:T(8,128)(2,1)} %bitcast.40, bf16[256,4,896]{2,1,0:T(4,128)(2,1)S(1)} %copy-done.4), kind=kOutput, calls=%fused_computation.23 | convolution fusion | flops 1409482752 | bytes 7733248 | tf_op jit(solution)/shard_map/srd,hsd->rh/dot_general | solution.py:64
  261.3 0.3 pad_maximum_fusion.3
  261.5 37.8 %all_to_all.17 = bf16[64,24,256]{2,1,0:T(8,128)(2,1)S(1)} all-to-all(bf16[64,24,256]{2,1,0:T(8,128)(2,1)S(1)} %pad_maximum_fusion.3), channel_id=1, replica_groups=mesh['dp'=2,'section'=4,'expert'=64] {'expert'}, dimensions={0} | all-to-all | bytes 1572864 | tf_op jit(solution)/shard_map/all_to_all | solution.py:71
  299.4 1.4 fusion.27
  300.7 1.1 copy.38
  301.8 9.6 %psum.7 = f32[128,8]{0,1:T(8,128)} all-reduce(f32[128,8]{0,1:T(8,128)S(1)} %get-tuple-element.12), channel_id=1, replica_groups=mesh['dp'=2,'section'=4,'expert'=64] {'section'}, use_global_device_ids=true, to_apply=%region_3.4 | all-reduce | flops 1024 | bytes 8192 | tf_op jit(solution)/shard_map/psum | solution.py:80
  311.5 2.2 copy.39
  (36 shorter events, 1.3 us)
Async XLA Ops:
  7.2 2.7 copy-start
  7.2 2.9 copy-start.6
  7.2 170.1 %all-gather.5.cloned.1.call-start = ((), (), s32[]{:S(2)}) async-start(), calls=%async_computation.5 | async-start | bytes 6881280 | tf_op jit(solution)/shard_map/all_gather | solution.py:59
  10.1 1.4 copy-start.5
  11.3 0.8 copy-start.7
  95.1 1.7 copy-start.1
  95.1 1.7 copy-start.8
  96.3 144.9 %all-gather.7.cloned.1.call-start = ((), (), s32[]{:S(2)}) async-start(), calls=%async_computation.6 | async-start | bytes 6881280 | tf_op jit(solution)/shard_map/all_gather | solution.py:59
  175.7 7.8 %copy-start.2 = (bf16[768,1152]{1,0:T(8,128)(2,1)}, bf16[768,1152]{1,0:T(8,128)(2,1)S(1)}, u32[]{:S(2)}) copy-start(bf16[768,1152]{1,0:T(8,128)(2,1)S(1)} %reshape.99) | copy-start | bytes 5308420
  177.1 134.4 %reduce-scatter.2.cloned.1.call-start = ((), (), s32[]{:S(2)}) async-start(), calls=%async_computation.4 | async-start | bytes 2752512 | tf_op jit(solution)/shard_map/reduce_scatter | solution.py:69
  249.0 1.5 copy-start.3
  252.0 5.0 %copy-start.4 = (bf16[256,4,896]{2,1,0:T(4,128)(2,1)S(1)}, bf16[256,4,896]{2,1,0:T(4,128)(2,1)}, u32[]{:S(2)}) copy-start(bf16[256,4,896]{2,1,0:T(4,128)(2,1)} %reshape_squeeze.3) | copy-start | bytes 5505028
  261.2 38.2 %copy-start.9 = (f32[128,8]{0,1:T(8,128)S(1)}, f32[128,8]{0,1:T(8,128)}, u32[]{:S(2)}) copy-start(f32[128,8]{0,1:T(8,128)} %param.7) | copy-start | bytes 12292
Sparse Core Ops, SparseCore 0:
  96.4 63.8 all-gather.4
  177.2 63.9 all-gather.6
  249.2 18.2 reduce-scatter.1

commit v7 on v6

--- a/solution.py
+++ b/solution.py
@@ -41,13 +41,13 @@
     )
     flat_pos = position.reshape(pair_count)
     w_local = w_down[0].reshape(hidden_slice, n_section, d_slice)
-    chunks = 2
-    step = capacity // chunks
+    bounds = [(lo, min(lo + 8, capacity)) for lo in range(0, capacity, 8)]
     received = []
-    for c in range(chunks):
+    for lo, hi in bounds:
+        step = hi - lo
         chunk_slots = (
             jnp.arange(experts, dtype=jnp.int32)[:, None] * capacity
-            + c * step
+            + lo
             + jnp.arange(step, dtype=jnp.int32)[None, :]
         ).reshape(experts * step)
         sel_c = (flat_pos[None, :] == chunk_slots[:, None]).astype(jnp.bfloat16)
@@ -57,10 +57,10 @@
             "expert", split_axis=0, concat_axis=0, tiled=True,
         ).reshape(experts * step, d_slice + hidden_slice)
         gathered = lax.all_gather(part[:, :d_slice], "section", axis=0, tiled=False)
-        received.append((part[:, d_slice:], gathered))
+        received.append((part[:, d_slice:], gathered, step))
     weight_acc = None
     returning = []
-    for recv_scaled, gathered in received:
+    for recv_scaled, gathered, step in received:
         unscaled = jnp.einsum("srd,hsd->rh", gathered, w_local, preferred_element_type=jnp.float32)
         returning.append(unscaled.astype(jnp.bfloat16).reshape(experts, step, hidden_slice))
         term = jnp.einsum("rh,srd->hsd", recv_scaled, gathered, preferred_element_type=jnp.float32)

time: 321 us -> 289 us (0.900)
  blocking collectives: 191 us -> 174 us
  local copies, waits for them, and re-layouts: 23 us -> 15.5 us
  waiting for transfers between devices: 57.7 us -> 50.9 us
    all_to_all x2 -> x3, blocking collectives: 143 us -> 126 us  [local(): lax.all_to_all(send_c.reshape(experts, step, d_slice + hidden_slice), 'ex...]
    reshape x6 -> x0, local copies, waits for them, and re-layouts: 10.1 us -> none  [the longest x2 5.08 us: local(): part = lax.all_to_all(send_c.reshape(experts, step, d_slice + hidden_slic...]
    all_gather x2 -> x3, waiting for transfers between devices: 57.7 us -> 50.8 us  [local(): gathered = lax.all_gather(part[:, :d_slice], 'section', axis=0, tiled=False)]
    dot_general x2 -> x3, matrix products: 11.6 us -> 15.6 us  [local(): jnp.einsum('rh,srd->hsd', recv_scaled, gathered, preferred_element_type=j...]
    dot_general x2 -> x3, matrix products: 9.06 us -> 6.21 us  [local(): jnp.einsum('srd,hsd->rh', gathered, w_local, preferred_element_type=jnp.f...]
    dot_general x2 -> x3, matrix products: 8.56 us -> 6.79 us  [local(): jnp.dot(sel_c, payload, preferred_element_type=jnp.float32)]
  transfers between devices with their start and end apart: 3 -> 4, of which waited for: 1 -> 2; matrix products, arithmetic and copies ran while one was open for 10% -> 10% of each run, Pallas kernels for 0% -> 0%
where the time goes in v7:
time: 289 us; the launch traced here: 288 us
  blocking collectives  174 us (60%)
  waiting for transfers between devices  50.9 us (18%)
  matrix products  30.1 us (10%)
  local copies, waits for them, and re-layouts  15.5 us (5%)
  between operations  13.9 us (5%)
  other arithmetic  3.75 us (1%)
    all_to_all x3, blocking collectives, local(): lax.all_to_all(send_c.reshape(experts, step, d_slice + hidden_slice), 'ex...  126 us
    all_gather x3, waiting for transfers between devices, local(): gathered = lax.all_gather(part[:, :d_slice], 'section', axis=0, tiled=False)  50.8 us
    all_to_all x1, blocking collectives, local(): lax.all_to_all(returning, 'expert', split_axis=0, concat_axis=0, tiled=True)  38 us
    dot_general x3, matrix products, local(): jnp.einsum('rh,srd->hsd', recv_scaled, gathered, preferred_element_type=j...  15.6 us
    psum x1, blocking collectives, local(): grad_gates = lax.psum(gate_share, 'section')  9.36 us
    dot_general x3, matrix products, local(): jnp.dot(sel_c, payload, preferred_element_type=jnp.float32)  6.79 us
    unnamed x18, local copies, waits for them, and re-layouts  6.4 us
    dot_general x3, matrix products, local(): jnp.einsum('srd,hsd->rh', gathered, w_local, preferred_element_type=jnp.f...  6.21 us
  transfers between devices with their start and end apart: 4, of which 2 were waited for; matrix products, arithmetic and copies ran while one was open for 10% of the time, Pallas kernels for 0%

profile of v7, /device:TPU:16, one launch (start us, length us, event | category | flops | bytes accessed | tf_op | source)
XLA Modules:
  0.0 288.2 jit_solution(6792181099082753177)
XLA Ops:
  7.2 0.8 fusion.53
  8.1 0.7 select_reduce_fusion
  8.9 0.7 convert_add_fusion
  9.8 1.3 fusion.43
  11.8 0.4 copy-done.6
  12.2 1.6 fusion.4
  13.7 49.3 %all_to_all.20 = bf16[64,8,1152]{2,1,0:T(8,128)(2,1)S(1)} all-to-all(bf16[64,8,1152]{2,1,0:T(8,128)(2,1)S(1)} %fusion.4), channel_id=1, replica_groups=mesh['dp'=2,'section'=4,'expert'=64] {'expert'}, dimensions={0} | all-to-all | bytes 2359296 | tf_op jit(solution)/shard_map/all_to_all | solution.py:55
  63.0 1.0 slice.24
  64.3 2.6 fusion.5
  66.9 38.7 %all_to_all.21 = bf16[64,8,1152]{2,1,0:T(8,128)(2,1)} all-to-all(bf16[64,8,1152]{2,1,0:T(8,128)(2,1)S(1)} %fusion.5), channel_id=1, replica_groups=mesh['dp'=2,'section'=4,'expert'=64] {'expert'}, dimensions={0} | all-to-all | bytes 2359296 | tf_op jit(solution)/shard_map/all_to_all | solution.py:55
  105.6 2.2 slice.25
  108.0 2.6 fusion.6
  110.6 38.3 %all_to_all.22 = bf16[64,8,1152]{2,1,0:T(8,128)(2,1)S(1)} all-to-all(bf16[64,8,1152]{2,1,0:T(8,128)(2,1)S(1)} %fusion.6), channel_id=1, replica_groups=mesh['dp'=2,'section'=4,'expert'=64] {'expert'}, dimensions={0} | all-to-all | bytes 2359296 | tf_op jit(solution)/shard_map/all_to_all | solution.py:55
  149.0 1.0 slice.26
  150.3 5.1 %fusion.52 = f32[256,4,896]{2,0,1:T(8,128)} fusion(bf16[4,512,896]{2,1,0:T(8,128)(2,1)} %bitcast.75, bf16[512,1152]{1,0:T(8,128)(2,1)S(1)} %bitcast.74), kind=kOutput, calls=%fused_computation.48 | convolution fusion | flops 939524096 | bytes 7602176 | tf_op jit(solution)/shard_map/rh,srd->hsd/dot_general | solution.py:66
  155.4 3.7 %all-gather.9.cloned.1.call-done = bf16[2048,896]{1,0:T(8,128)(2,1)} async-done(((bf16[512,896]{1,0:T(8,128)(2,1)}), bf16[2048,896]{1,0:T(8,128)(2,1)}) %all-gather.9.cloned.1.call-update) | async-done | bytes 3670032 | tf_op jit(solution)/shard_map/all_gather | solution.py:59
  159.1 5.1 %fusion.51 = f32[256,4,896]{2,0,1:T(8,128)} fusion(bf16[4,512,896]{2,1,0:T(8,128)(2,1)} %bitcast.77, bf16[512,1152]{1,0:T(8,128)(2,1)} %bitcast.9), kind=kOutput, calls=%fused_computation.46 | convolution fusion | flops 939524096 | bytes 7602176 | tf_op jit(solution)/shard_map/rh,srd->hsd/dot_general | solution.py:66
  164.1 47.1 %all-gather.11.cloned.1.call-done = bf16[2048,896]{1,0:T(8,128)(2,1)} async-done(((bf16[512,896]{1,0:T(8,128)(2,1)}), bf16[2048,896]{1,0:T(8,128)(2,1)}) %all-gather.11.cloned.1.call-update) | async-done | bytes 3670032 | tf_op jit(solution)/shard_map/all_gather | solution.py:59
  211.3 5.4 %add_convert_fusion = bf16[256,4,896]{2,0,1:T(8,128)(2,1)S(1)} fusion(f32[256,4,896]{2,0,1:T(8,128)} %fusion.52, f32[256,4,896]{2,0,1:T(8,128)} %fusion.51, bf16[4,512,896]{2,1,0:T(8,128)(2,1)} %bitcast.79, bf16[512,1152]{1,0:T(8,128)(2,1)S(1)} %bitcast.72), kind=kOutput, calls=%fused_computation.3 | convolution fusion | flops 942276608 | bytes 13107200 | tf_op jit(solution)/shard_map/rh,srd->hsd/dot_general | solution.py:66
  216.7 2.5 copy.44
  219.2 1.5 copy-done.3
  220.6 1.4 reshape_squeeze.3
  222.1 3.9 %fusion.40 = bf16[64,8,256]{2,1,0:T(8,128)(2,1)S(1)} fusion(bf16[4,512,896]{2,1,0:T(8,128)(2,1)} %bitcast.80, bf16[256,4,896]{2,1,0:T(4,128)(2,1)} %reshape_squeeze.3), kind=kOutput, calls=%fused_computation.31 | convolution fusion | flops 939655168 | bytes 5767168 | tf_op jit(solution)/shard_map/srd,hsd->rh/dot_general | solution.py:64
  226.0 0.3 copy-done.4
  226.3 1.1 fusion.37
  227.5 0.9 copy-done.1
  228.4 1.1 fusion.34
  229.6 38.0 %all_to_all.23 = bf16[64,24,256]{2,1,0:T(8,128)(2,1)S(1)} all-to-all(bf16[64,24,256]{2,1,0:T(8,128)(2,1)S(1)} %pad_maximum_fusion.1), channel_id=1, replica_groups=mesh['dp'=2,'section'=4,'expert'=64] {'expert'}, dimensions={0} | all-to-all | bytes 1572864 | tf_op jit(solution)/shard_map/all_to_all | solution.py:71
  267.6 1.4 fusion.44
  269.0 1.1 copy.45
  270.1 9.4 %psum.7 = f32[128,8]{0,1:T(8,128)} all-reduce(f32[128,8]{0,1:T(8,128)S(1)} %get-tuple-element.12), channel_id=1, replica_groups=mesh['dp'=2,'section'=4,'expert'=64] {'section'}, use_global_device_ids=true, to_apply=%region_3.4 | all-reduce | flops 1024 | bytes 8192 | tf_op jit(solution)/shard_map/psum | solution.py:80
  279.4 2.2 copy.46
  (37 shorter events, 1.9 us)
Async XLA Ops:
  7.2 4.2 %copy-start = (bf16[128,896]{1,0:T(8,128)(2,1)S(1)}, bf16[128,896]{1,0:T(8,128)(2,1)}, u32[]{:S(2)}) copy-start(bf16[128,896]{1,0:T(8,128)(2,1)} %param.5) | copy-start | bytes 688132
  7.2 143.1 %all-gather.7.cloned.1.call-start = ((), (), s32[]{:S(2)}) async-start(), calls=%async_computation.6 | async-start | bytes 4587520 | tf_op jit(solution)/shard_map/all_gather | solution.py:59
  11.4 0.8 copy-start.6
  64.0 95.0 %all-gather.9.cloned.1.call-start = ((), (), s32[]{:S(2)}) async-start(), calls=%async_computation.7 | async-start | bytes 4587520 | tf_op jit(solution)/shard_map/all_gather | solution.py:59
  107.8 103.5 %all-gather.11.cloned.1.call-start = ((), (), s32[]{:S(2)}) async-start(), calls=%async_computation.8 | async-start | bytes 4587520 | tf_op jit(solution)/shard_map/all_gather | solution.py:59
  150.0 129.4 %reduce-scatter.2.cloned.1.call-start = ((), (), s32[]{:S(2)}) async-start(), calls=%async_computation.5 | async-start | bytes 2752512 | tf_op jit(solution)/shard_map/reduce_scatter | solution.py:69
  219.1 1.5 copy-start.3
  222.1 3.9 %copy-start.2 = (bf16[2048,896]{1,0:T(8,128)(2,1)S(1)}, bf16[2048,896]{1,0:T(8,128)(2,1)}, u32[]{:S(2)}) copy-start(bf16[2048,896]{1,0:T(8,128)(2,1)} %all-gather.9.cloned.1.call-done) | copy-start | bytes 11010052
  222.1 4.3 %copy-start.4 = (bf16[256,4,896]{2,1,0:T(4,128)(2,1)S(1)}, bf16[256,4,896]{2,1,0:T(4,128)(2,1)}, u32[]{:S(2)}) copy-start(bf16[256,4,896]{2,1,0:T(4,128)(2,1)} %reshape_squeeze.3) | copy-start | bytes 5505028
  226.3 2.0 copy-start.1
  229.5 38.1 %copy-start.5 = (bf16[128,8,256]{2,1,0:T(8,128)(2,1)S(1)}, bf16[128,8,256]{2,1,0:T(8,128)(2,1)}, u32[]{:S(2)}) copy-start(bf16[128,8,256]{2,1,0:T(8,128)(2,1)} %param.8) | copy-start | bytes 1572868
  229.6 38.0 %copy-start.7 = (f32[128,8]{0,1:T(8,128)S(1)}, f32[128,8]{0,1:T(8,128)}, u32[]{:S(2)}) copy-start(f32[128,8]{0,1:T(8,128)} %param.7) | copy-start | bytes 12292
Sparse Core Ops, SparseCore 0:
  64.2 43.2 all-gather.6
  109.5 49.4 all-gather.8
  161.7 49.4 all-gather.10
  219.3 17.9 reduce-scatter.1

commit v8 on v7

--- a/solution.py
+++ b/solution.py
@@ -43,7 +43,7 @@
     w_local = w_down[0].reshape(hidden_slice, n_section, d_slice)
     bounds = [(lo, min(lo + 8, capacity)) for lo in range(0, capacity, 8)]
     received = []
-    for lo, hi in bounds:
+    for c, (lo, hi) in enumerate(bounds):
         step = hi - lo
         chunk_slots = (
             jnp.arange(experts, dtype=jnp.int32)[:, None] * capacity
@@ -56,7 +56,13 @@
             send_c.reshape(experts, step, d_slice + hidden_slice),
             "expert", split_axis=0, concat_axis=0, tiled=True,
         ).reshape(experts * step, d_slice + hidden_slice)
-        gathered = lax.all_gather(part[:, :d_slice], "section", axis=0, tiled=False)
+        if c == len(bounds) - 1 and c > 0:
+            spread = jnp.broadcast_to(
+                part[None, :, :d_slice], (n_section, experts * step, d_slice)
+            )
+            gathered = lax.all_to_all(spread, "section", split_axis=0, concat_axis=0, tiled=True)
+        else:
+            gathered = lax.all_gather(part[:, :d_slice], "section", axis=0, tiled=False)
         received.append((part[:, d_slice:], gathered, step))
     weight_acc = None
     returning = []

time: 289 us -> 276 us (0.955)
  waiting for transfers between devices: 50.9 us -> 32.3 us
  starting transfers between devices: 0.34 us -> 5.05 us
    all_gather x3 -> x2, waiting for transfers between devices: 50.8 us -> 0.02 us  [local(): gathered = lax.all_gather(part[:, :d_slice], 'section', axis=0, tiled=False)]
    all_to_all x0 -> x1, waiting for transfers between devices: none -> 32.2 us  [local(): lax.all_to_all(spread, 'section', split_axis=0, concat_axis=0, tiled=True)]
    all_to_all x0 -> x1, starting transfers between devices: none -> 4.75 us  [local(): lax.all_to_all(spread, 'section', split_axis=0, concat_axis=0, tiled=True)]
  transfers between devices with their start and end apart: 4 -> 4, of which waited for: 2 -> 1; matrix products, arithmetic and copies ran while one was open for 10% -> 11% of each run, Pallas kernels for 0% -> 0%
where the time goes in v8:
time: 276 us
  blocking collectives  174 us (63%)
  waiting for transfers between devices  32.3 us (12%)
  matrix products  30 us (11%)
  local copies, waits for them, and re-layouts  16.3 us (6%)
  between operations  13.9 us (5%)
  starting transfers between devices  5.05 us (2%)
  other arithmetic  3.75 us (1%)
    all_to_all x3, blocking collectives, local(): lax.all_to_all(send_c.reshape(experts, step, d_slice + hidden_slice), 'ex...  126 us
    all_to_all x1, blocking collectives, local(): lax.all_to_all(returning, 'expert', split_axis=0, concat_axis=0, tiled=True)  38.1 us
    all_to_all x1, waiting for transfers between devices, local(): lax.all_to_all(spread, 'section', split_axis=0, concat_axis=0, tiled=True)  32.2 us
    dot_general x3, matrix products, local(): jnp.einsum('rh,srd->hsd', recv_scaled, gathered, preferred_element_type=j...  15.5 us
    psum x1, blocking collectives, local(): grad_gates = lax.psum(gate_share, 'section')  9.98 us
    dot_general x3, matrix products, local(): jnp.dot(sel_c, payload, preferred_element_type=jnp.float32)  6.8 us
    dot_general x3, matrix products, local(): jnp.einsum('srd,hsd->rh', gathered, w_local, preferred_element_type=jnp.f...  6.2 us
    unnamed x18, local copies, waits for them, and re-layouts  6.01 us
  transfers between devices with their start and end apart: 4, of which 1 were waited for; matrix products, arithmetic and copies ran while one was open for 11% of the time, Pallas kernels for 0%

profile of v8, /device:TPU:16, one launch (start us, length us, event | category | flops | bytes accessed | tf_op | source)
XLA Modules:
  0.0 275.6 jit_solution(4409845331919044736)
XLA Ops:
  7.2 0.8 fusion.53
  8.1 0.7 select_reduce_fusion
  8.9 0.7 convert_add_fusion
  10.0 1.3 fusion.43
  11.2 0.3 copy.77
  11.8 1.6 fusion.5
  13.4 49.3 %all_to_all.25 = bf16[64,8,1152]{2,1,0:T(8,128)(2,1)S(1)} all-to-all(bf16[64,8,1152]{2,1,0:T(8,128)(2,1)S(1)} %fusion.5), channel_id=1, replica_groups=mesh['dp'=2,'section'=4,'expert'=64] {'expert'}, dimensions={0} | all-to-all | bytes 2359296 | tf_op jit(solution)/shard_map/all_to_all | solution.py:55
  62.6 1.0 slice.25
  63.9 2.6 fusion.4
  66.5 38.7 %all_to_all.26 = bf16[64,8,1152]{2,1,0:T(8,128)(2,1)} all-to-all(bf16[64,8,1152]{2,1,0:T(8,128)(2,1)S(1)} %fusion.4), channel_id=1, replica_groups=mesh['dp'=2,'section'=4,'expert'=64] {'expert'}, dimensions={0} | all-to-all | bytes 2359296 | tf_op jit(solution)/shard_map/all_to_all | solution.py:55
  105.2 2.2 slice.24
  107.5 2.6 fusion.6
  110.2 38.3 %all_to_all.27 = bf16[64,8,1152]{2,1,0:T(8,128)(2,1)S(1)} all-to-all(bf16[64,8,1152]{2,1,0:T(8,128)(2,1)S(1)} %fusion.6), channel_id=1, replica_groups=mesh['dp'=2,'section'=4,'expert'=64] {'expert'}, dimensions={0} | all-to-all | bytes 2359296 | tf_op jit(solution)/shard_map/all_to_all | solution.py:55
  148.6 2.2 broadcast_in_dim.19
  150.8 4.7 %all-to-all-start.3 = ((bf16[4,512,896]{2,1,0:T(8,128)(2,1)}), bf16[4,512,896]{2,1,0:T(8,128)(2,1)}, u32[]{:S(2)}, u32[]{:S(2)}) async-start(bf16[4,512,896]{2,1,0:T(8,128)(2,1)} %broadcast_in_dim.19), calls=%async_computation.3 | async-start | bytes 7340032 | tf_op jit(solution)/shard_map/all_to_all | solution.py:63
  155.8 5.0 %fusion.51 = f32[256,4,896]{2,0,1:T(8,128)} fusion(bf16[4,512,896]{2,1,0:T(8,128)(2,1)} %bitcast.74, bf16[512,1152]{1,0:T(8,128)(2,1)S(1)} %bitcast.73), kind=kOutput, calls=%fused_computation.46 | convolution fusion | flops 939524096 | bytes 7602176 | tf_op jit(solution)/shard_map/rh,srd->hsd/dot_general | solution.py:72
  160.8 5.1 %fusion.52 = f32[256,4,896]{2,0,1:T(8,128)} fusion(bf16[4,512,896]{2,1,0:T(8,128)(2,1)} %bitcast.76, bf16[512,1152]{1,0:T(8,128)(2,1)} %bitcast.4), kind=kOutput, calls=%fused_computation.48 | convolution fusion | flops 939524096 | bytes 7602176 | tf_op jit(solution)/shard_map/rh,srd->hsd/dot_general | solution.py:72
  165.8 32.2 %all-to-all-done.3 = bf16[4,512,896]{2,1,0:T(8,128)(2,1)} async-done(((bf16[4,512,896]{2,1,0:T(8,128)(2,1)}), bf16[4,512,896]{2,1,0:T(8,128)(2,1)}, u32[]{:S(2)}, u32[]{:S(2)}) %all-to-all-start.3) | async-done | bytes 3670048 | tf_op jit(solution)/shard_map/all_to_all | solution.py:63
  198.0 5.4 %add_convert_fusion = bf16[256,4,896]{2,0,1:T(8,128)(2,1)S(1)} fusion(f32[256,4,896]{2,0,1:T(8,128)} %fusion.52, f32[256,4,896]{2,0,1:T(8,128)} %fusion.51, bf16[4,512,896]{2,1,0:T(8,128)(2,1)} %all-to-all-done.3, bf16[512,1152]{1,0:T(8,128)(2,1)S(1)} %bitcast.71), kind=kOutput, calls=%fused_computation.3 | convolution fusion | flops 942276608 | bytes 13107200 | tf_op jit(solution)/shard_map/rh,srd->hsd/dot_general | solution.py:72
  203.4 2.4 copy.44
  205.9 1.5 copy-done.3
  207.4 1.5 reshape_squeeze.3
  208.8 3.9 %fusion.40 = bf16[64,8,256]{2,1,0:T(8,128)(2,1)S(1)} fusion(bf16[4,512,896]{2,1,0:T(8,128)(2,1)} %all-to-all-done.3, bf16[256,4,896]{2,1,0:T(4,128)(2,1)} %reshape_squeeze.3), kind=kOutput, calls=%fused_computation.31 | convolution fusion | flops 939655168 | bytes 5767168 | tf_op jit(solution)/shard_map/srd,hsd->rh/dot_general | solution.py:70
  212.7 0.3 copy-done.4
  213.1 1.2 fusion.37
  214.2 0.9 copy-done.2
  215.1 1.1 fusion.34
  216.3 38.1 %all_to_all.28 = bf16[64,24,256]{2,1,0:T(8,128)(2,1)S(1)} all-to-all(bf16[64,24,256]{2,1,0:T(8,128)(2,1)S(1)} %pad_maximum_fusion.1), channel_id=1, replica_groups=mesh['dp'=2,'section'=4,'expert'=64] {'expert'}, dimensions={0} | all-to-all | bytes 1572864 | tf_op jit(solution)/shard_map/all_to_all | solution.py:77
  254.4 1.4 fusion.44
  255.8 1.1 copy.45
  256.9 10.0 %psum.7 = f32[128,8]{0,1:T(8,128)} all-reduce(f32[128,8]{0,1:T(8,128)S(1)} %get-tuple-element.12), channel_id=1, replica_groups=mesh['dp'=2,'section'=4,'expert'=64] {'section'}, use_global_device_ids=true, to_apply=%region_3.4 | all-reduce | flops 1024 | bytes 8192 | tf_op jit(solution)/shard_map/psum | solution.py:86
  266.9 2.2 copy.46
  (37 shorter events, 1.6 us)
Async XLA Ops:
  7.2 4.4 %copy-start = (bf16[128,896]{1,0:T(8,128)(2,1)S(1)}, bf16[128,896]{1,0:T(8,128)(2,1)}, u32[]{:S(2)}) copy-start(bf16[128,896]{1,0:T(8,128)(2,1)} %param.5) | copy-start | bytes 688132
  7.2 148.6 %all-gather.7.cloned.1.call-start = ((), (), s32[]{:S(2)}) async-start(), calls=%async_computation.8 | async-start | bytes 4587520 | tf_op jit(solution)/shard_map/all_gather | solution.py:65
  11.5 1.8 copy-start.6
  63.7 97.1 %all-gather.5.cloned.1.call-start = ((), (), s32[]{:S(2)}) async-start(), calls=%async_computation.7 | async-start | bytes 4587520 | tf_op jit(solution)/shard_map/all_gather | solution.py:65
  150.8 47.3 %all-to-all-start.3 = ((bf16[4,512,896]{2,1,0:T(8,128)(2,1)}), bf16[4,512,896]{2,1,0:T(8,128)(2,1)}, u32[]{:S(2)}, u32[]{:S(2)}) async-start(bf16[4,512,896]{2,1,0:T(8,128)(2,1)} %broadcast_in_dim.19), calls=%async_computation.3 | async-start | bytes 7340032 | tf_op jit(solution)/shard_map/all_to_all | solution.py:63
  155.5 111.4 %reduce-scatter.2.cloned.1.call-start = ((), (), s32[]{:S(2)}) async-start(), calls=%async_computation.6 | async-start | bytes 2752512 | tf_op jit(solution)/shard_map/reduce_scatter | solution.py:75
  205.9 1.5 copy-start.3
  208.8 3.9 %copy-start.1 = (bf16[2048,896]{1,0:T(8,128)(2,1)S(1)}, bf16[2048,896]{1,0:T(8,128)(2,1)}, u32[]{:S(2)}) copy-start(bf16[2048,896]{1,0:T(8,128)(2,1)} %all-gather.7.cloned.1.call-done) | copy-start | bytes 11010052
  208.8 4.3 %copy-start.4 = (bf16[256,4,896]{2,1,0:T(4,128)(2,1)S(1)}, bf16[256,4,896]{2,1,0:T(4,128)(2,1)}, u32[]{:S(2)}) copy-start(bf16[256,4,896]{2,1,0:T(4,128)(2,1)} %reshape_squeeze.3) | copy-start | bytes 5505028
  213.1 2.0 copy-start.2
  216.3 38.2 %copy-start.5 = (bf16[128,8,256]{2,1,0:T(8,128)(2,1)S(1)}, bf16[128,8,256]{2,1,0:T(8,128)(2,1)}, u32[]{:S(2)}) copy-start(bf16[128,8,256]{2,1,0:T(8,128)(2,1)} %param.8) | copy-start | bytes 1572868
  216.3 38.1 %copy-start.7 = (f32[128,8]{0,1:T(8,128)S(1)}, f32[128,8]{0,1:T(8,128)}, u32[]{:S(2)}) copy-start(f32[128,8]{0,1:T(8,128)} %param.7) | copy-start | bytes 12292
Sparse Core Ops, SparseCore 0:
  63.8 43.2 all-gather.6
  109.2 50.6 all-gather.4
  206.0 17.6 reduce-scatter.1
